TPU v7x, 32 devices: a whole 2x2x4 slice. The times are simulated.
32 devices in a mesh: groups: 2 (over y), tm: 4 (over z), space: 2 (over x), dp: 2 (over core).
Axes of the slice: x: 2, y: 2, z: 4, core: 2. Of those that a mesh axis runs over, the one named last changes fastest.
Arguments:
- video_input: bfloat16 [4, 4, 8, 256, 96], P(('groups', 'dp'), 'tm', 'space'), parts along dimension 0, may hold values from -48 to 48
- out_cotangent: bfloat16 [4, 4, 8, 256, 96], P(('groups', 'dp'), 'tm', 'space'), parts along dimension 0, may hold values from -6 to 6
- conv_weight: bfloat16 [3, 3, 3, 96, 96], replicated, may hold values from -0.125 to 0.125
- sketch_signs: int32 [2, 96, 32], replicated, may hold values from 0 to 1
Outputs:
- input_grad: bfloat16 [4, 4, 8, 256, 96], P(('groups', 'dp'), 'tm', 'space'), parts along dimension 0
- weight_grad: float32 [6, 3, 3, 96, 96], P('groups'), parts along dimension 0
- sketches: float32 [4, 96, 32], P('groups'), parts along dimension 0
There are 2 independent parts, one for each index of `groups`. A program takes and returns all parts, laid end to end along the dimension named above; an argument that names none is the same for every part. Nothing has to cross between parts.
All inputs are finite; a program needn't handle non-finite values.
Results may differ from a plain program's by a relative error of at most 0.0025.
Values may be sent and summed in bfloat16 or wider, within the bound.
No kernel may reach another device: no remote copies, remote signals or barrier semaphores. Data moves between devices by JAX's collectives and lax.ppermute only.
A program may use at most 64 MiB of HBM per device.

v0:
```python
import jax
import jax.numpy as jnp
from jax import lax
from jax.sharding import PartitionSpec as P


def padded(value, sides, width):
    for axis, dim in sides:
        peers, length = (lax.axis_size(axis), value.shape[dim])
        up = [(i, (i + 1) % peers) for i in range(peers - 1)]
        down = [(j, i) for i, j in up]
        last = lax.slice_in_dim(value, length - width, length, axis=dim)
        leading = lax.slice_in_dim(value, 0, width, axis=dim)
        before = lax.ppermute(last, axis, up)
        after = lax.ppermute(leading, axis, down)
        value = jnp.concatenate([before, value, after], axis=dim)
    return value


def passed_along(block, axis, distance):
    devices = range(lax.axis_size(axis))
    route = [(i - distance, i) for i in devices if i - distance in devices]
    return lax.ppermute(block, axis, route)


def silu_slope(value):
    sig = jax.nn.sigmoid(value)
    return sig * (1.0 + value * (1.0 - sig))


def pad_columns(field):
    return jnp.pad(field, ((0, 0), (0, 0), (1, 1), (0, 0)))


def contract_rows(left, right):
    return lax.dot_general(
        left, right, (((0,), (0,)), ((), ())), preferred_element_type=jnp.float32
    )


def on_device(video_input, out_cotangent, conv_weight, sketch_signs):
    xin = video_input[:, 0]
    grad_out = out_cotangent[:, 0]
    batch, rows, width, chans = xin.shape
    count = batch * rows * width
    hidden = jax.nn.silu(xin.astype(jnp.float32)).astype(jnp.bfloat16)
    hid_flat = hidden.reshape(count, chans)
    grad_flat = grad_out.reshape(count, chans)
    grad_rows = padded(grad_out, (("space", 1),), 1)
    grad_frames = [pad_columns(grad_rows)]
    for lag in (1, 2):
        grad_frames.append(pad_columns(passed_along(grad_rows, "tm", -lag)))
    hid_rows = padded(hidden, (("space", 1),), 1)
    hid_frames = [pad_columns(hid_rows)]
    for lag in (1, 2):
        hid_frames.append(pad_columns(passed_along(hid_rows, "tm", lag)))
    grad_hidden = jnp.zeros((count, chans), jnp.float32)
    kernel_terms = []
    for a in range(3):
        for b in range(3):
            source = grad_frames[2 - a]
            slab = jnp.concatenate(
                [source[:, 2 - b : 2 - b + rows, 2 - e : 2 - e + width, :] for e in range(3)],
                axis=-1,
            ).reshape(count, 3 * chans)
            weight_mat = jnp.transpose(conv_weight[a, b], (0, 2, 1)).reshape(3 * chans, chans)
            grad_hidden = grad_hidden + jnp.dot(
                slab, weight_mat, preferred_element_type=jnp.float32
            )
            earlier = hid_frames[2 - a]
            hid_slab = jnp.concatenate(
                [earlier[:, b : b + rows, e : e + width, :] for e in range(3)], axis=-1
            ).reshape(count, 3 * chans)
            kernel_terms.append(contract_rows(hid_slab, grad_flat).reshape(3, chans, chans))
    kernel_local = jnp.stack(kernel_terms).reshape(3, 3, 3, chans, chans)
    xflat = xin.reshape(count, chans).astype(jnp.float32)
    input_grad = (grad_hidden * silu_slope(xflat)).astype(jnp.bfloat16)
    input_grad = input_grad.reshape(batch, 1, rows, width, chans)
    omega = (2 * sketch_signs - 1).astype(jnp.float32)
    cov_hidden = contract_rows(hid_flat, hid_flat)
    cov_grad = contract_rows(grad_flat, grad_flat)
    sketch_terms = jnp.stack(
        [
            jnp.dot(cov_hidden, omega[0], precision=lax.Precision.HIGHEST),
            jnp.dot(cov_grad, omega[1], precision=lax.Precision.HIGHEST),
        ]
    )
    total_pixels = (
        count
        * video_input.shape[1]
        * lax.axis_size("tm")
        * lax.axis_size("space")
        * lax.axis_size("dp")
    )
    sketch_total = lax.psum(sketch_terms, ("tm", "space", "dp"))
    kernel_total = lax.psum(kernel_local, ("tm", "space", "dp"))
    sketches = sketch_total / jnp.float32(total_pixels)
    weight_grad = kernel_total * (1.0 / jnp.sqrt(jnp.float32(total_pixels)))
    return (input_grad, weight_grad, sketches)


def solution(mesh):
    in_specs = (
        P(("groups", "dp"), "tm", "space", None, None),
        P(("groups", "dp"), "tm", "space", None, None),
        P(),
        P(),
    )
    out_specs = (
        P(("groups", "dp"), "tm", "space", None, None),
        P("groups", None, None, None, None),
        P("groups", None, None),
    )
    return jax.shard_map(
        on_device, mesh=mesh, in_specs=in_specs, out_specs=out_specs, check_vma=False
    )
```

profile of v0, /device:TPU:0, one launch (start us, length us, event | category | flops | bytes accessed | tf_op | source)
XLA Modules:
  0.0 231.1 jit_solution(7625184018858395198)
XLA Ops:
  7.2 0.9 fusion.34
  8.2 1.3 collective-permute-start.1
  9.4 4.9 %collective-permute-start = (bf16[1,1,256,96]{2,3,1,0:T(8,128)(2,1)S(1)}, bf16[1,1,256,96]{2,3,1,0:T(8,128)(2,1)S(1)}, u32[]{:S(2)}, u32[]{:S(2)}) collective-permute-start(bf16[1,1,256,96]{2,3,1,0:T(8,128)(2,1)S(1)} %get-tuple-element.72), channel_id=1, source_target_pairs={{0,2},{1,3},{4,6},{5,7},{8,10},{9,11},{12,14},{13,15},{16,18},{17,... | collective-permute-start | bytes 147464 | tf_op jit(solution)/shard_map/ppermute | solution.py:14
  14.3 1.0 fusion.27
  15.4 1.3 collective-permute-start.5
  16.7 4.5 %collective-permute-start.4 = (bf16[1,1,256,96]{2,3,1,0:T(8,128)(2,1)S(1)}, bf16[1,1,256,96]{2,3,1,0:T(8,128)(2,1)S(1)}, u32[]{:S(2)}, u32[]{:S(2)}) collective-permute-start(bf16[1,1,256,96]{2,3,1,0:T(8,128)(2,1)S(1)} %get-tuple-element.68), channel_id=1, source_target_pairs={{0,2},{1,3},{4,6},{5,7},{8,10},{9,11},{12,14},{13,15},{16,18},{17,... | collective-permute-start | bytes 147464 | tf_op jit(solution)/shard_map/ppermute | solution.py:14
  21.2 1.1 copy.31
  22.9 0.6 copy-done.5
  23.7 0.5 copy-done.18
  24.6 59.7 %psum.15 = f32[2,96,32]{1,2,0:T(8,128)S(1)} all-reduce(f32[2,96,32]{1,2,0:T(8,128)S(1)} %pad_maximum_fusion.19), channel_id=1, replica_groups=mesh['groups'=2,'tm'=4,'space'=2,'dp'=2] {'tm','space','dp'}, use_global_device_ids=true, to_apply=%region_1.2 | all-reduce | flops 6144 | bytes 49152 | tf_op jit(solution)/shard_map/psum | solution.py:95
  84.3 0.6 broadcast_multiply_fusion.1
  85.1 0.7 copy.43
  85.8 0.7 copy.44
  86.6 0.7 copy.45
  87.3 0.7 copy.46
  88.0 0.7 copy.47
  88.8 0.7 copy.48
  89.5 0.7 copy.49
  90.2 0.7 copy.50
  91.1 0.7 copy.60
  91.8 0.7 copy.51
  92.5 1.3 collective-permute-start.2
  93.8 1.3 collective-permute-start.3
  95.6 6.1 %collective-permute-start.6 = (bf16[1,6,256,96]{2,3,1,0:T(8,128)(2,1)S(1)}, bf16[1,6,256,96]{2,3,1,0:T(8,128)(2,1)S(1)}, u32[]{:S(2)}, u32[]{:S(2)}) collective-permute-start(bf16[1,6,256,96]{2,3,1,0:T(8,128)(2,1)S(1)} %pad_maximum_fusion.18), channel_id=1, source_target_pairs={{0,8},{4,12},{1,9},{5,13},{2,10},{6,14},{3,11},{7,15},{16,24},{20,... | collective-permute-start | bytes 884744 | tf_op jit(solution)/shard_map/ppermute | solution.py:23
  101.7 4.1 %collective-permute-start.7 = (bf16[1,6,256,96]{2,3,1,0:T(8,128)(2,1)S(1)}, bf16[1,6,256,96]{2,3,1,0:T(8,128)(2,1)S(1)}, u32[]{:S(2)}, u32[]{:S(2)}) collective-permute-start(bf16[1,6,256,96]{2,3,1,0:T(8,128)(2,1)S(1)} %pad_maximum_fusion.18), channel_id=1, source_target_pairs={{0,4},{4,8},{8,12},{1,5},{5,9},{9,13},{2,6},{6,10},{10,14},{3,7},{... | collective-permute-start | bytes 884744 | tf_op jit(solution)/shard_map/ppermute | solution.py:23
  106.9 0.5 copy.23
  107.7 0.7 copy.61
  108.5 0.7 copy.59
  109.7 0.9 copy.62
  111.2 0.5 copy.41
  113.4 0.5 copy.11
  114.0 0.5 copy.13
  114.6 0.5 copy.15
  115.1 0.5 copy.17
  115.7 0.5 copy.19
  116.2 0.9 copy.56
  117.6 0.9 copy.57
  118.6 0.5 copy.32
  119.1 0.5 copy.33
  119.8 0.5 copy.34
  120.4 0.5 pad_slice_fusion.7
  120.9 0.5 copy.35
  121.5 0.7 copy.36
  125.8 1.1 copy-done.3
  126.9 1.2 fusion.35
  132.4 0.7 copy.42
  133.1 88.6 %all-reduce.8.cloned.1.call-done = f32[3,3,3,96,96]{4,3,2,1,0:T(8,128)} async-done(((f32[3,3,3,96,96]{4,3,2,1,0:T(8,128)}), f32[3,3,3,96,96]{4,3,2,1,0:T(8,128)}) %all-reduce.8.cloned.1.call-update) | async-done | bytes 995344 | tf_op jit(solution)/shard_map/psum | solution.py:96
  221.7 2.5 %broadcast_multiply_fusion = f32[3,3,3,96,96]{4,3,2,1,0:T(8,128)} fusion(f32[3,3,3,96,96]{4,3,2,1,0:T(8,128)} %all-reduce.8.cloned.1.call-done), kind=kLoop, calls=%fused_computation.32 | loop fusion | flops 248832 | bytes 1990656 | tf_op jit(solution)/shard_map/mul | solution.py:98
  (116 shorter events, 15.2 us)
Async XLA Ops:
  7.2 15.2 %copy-start = (bf16[1,1,4,256,96]{3,4,2,1,0:T(8,128)(2,1)S(1)}, bf16[1,1,4,256,96]{3,4,2,1,0:T(8,128)(2,1)}, u32[]{:S(2)}) copy-start(bf16[1,1,4,256,96]{3,4,2,1,0:T(8,128)(2,1)} %param.5) | copy-start | bytes 589828
  7.2 15.4 %copy-start.4 = (bf16[1,1,4,256,96]{3,4,2,1,0:T(8,128)(2,1)S(1)}, bf16[1,1,4,256,96]{3,4,2,1,0:T(8,128)(2,1)}, u32[]{:S(2)}) copy-start(bf16[1,1,4,256,96]{3,4,2,1,0:T(8,128)(2,1)} %param.4) | copy-start | bytes 589828
  7.2 214.5 %all-reduce.8.cloned.1.call-start = ((), (), s32[]{:S(2)}) async-start(), calls=%async_computation | async-start | bytes 2654208 | tf_op jit(solution)/shard_map/psum | solution.py:96
  8.2 84.3 %collective-permute-start.1 = (bf16[1,1,256,96]{2,3,1,0:T(8,128)(2,1)S(1)}, bf16[1,1,256,96]{2,3,1,0:T(8,128)(2,1)S(1)}, u32[]{:S(2)}, u32[]{:S(2)}) collective-permute-start(bf16[1,1,256,96]{2,3,1,0:T(8,128)(2,1)S(1)} %get-tuple-element.73), channel_id=1, source_target_pairs={{2,0},{3,1},{6,4},{7,5},{10,8},{11,9},{14,12},{15,13},{18,16},{19,... | collective-permute-start | bytes 147464 | tf_op jit(solution)/shard_map/ppermute | solution.py:15
  9.4 83.1 %collective-permute-start = (bf16[1,1,256,96]{2,3,1,0:T(8,128)(2,1)S(1)}, bf16[1,1,256,96]{2,3,1,0:T(8,128)(2,1)S(1)}, u32[]{:S(2)}, u32[]{:S(2)}) collective-permute-start(bf16[1,1,256,96]{2,3,1,0:T(8,128)(2,1)S(1)} %get-tuple-element.72), channel_id=1, source_target_pairs={{0,2},{1,3},{4,6},{5,7},{8,10},{9,11},{12,14},{13,15},{16,18},{17,... | collective-permute-start | bytes 147464 | tf_op jit(solution)/shard_map/ppermute | solution.py:14
  15.4 80.2 %collective-permute-start.5 = (bf16[1,1,256,96]{2,3,1,0:T(8,128)(2,1)S(1)}, bf16[1,1,256,96]{2,3,1,0:T(8,128)(2,1)S(1)}, u32[]{:S(2)}, u32[]{:S(2)}) collective-permute-start(bf16[1,1,256,96]{2,3,1,0:T(8,128)(2,1)S(1)} %get-tuple-element.69), channel_id=1, source_target_pairs={{2,0},{3,1},{6,4},{7,5},{10,8},{11,9},{14,12},{15,13},{18,16},{19,... | collective-permute-start | bytes 147464 | tf_op jit(solution)/shard_map/ppermute | solution.py:15
  16.7 78.9 %collective-permute-start.4 = (bf16[1,1,256,96]{2,3,1,0:T(8,128)(2,1)S(1)}, bf16[1,1,256,96]{2,3,1,0:T(8,128)(2,1)S(1)}, u32[]{:S(2)}, u32[]{:S(2)}) collective-permute-start(bf16[1,1,256,96]{2,3,1,0:T(8,128)(2,1)S(1)} %get-tuple-element.68), channel_id=1, source_target_pairs={{0,2},{1,3},{4,6},{5,7},{8,10},{9,11},{12,14},{13,15},{16,18},{17,... | collective-permute-start | bytes 147464 | tf_op jit(solution)/shard_map/ppermute | solution.py:14
  22.3 1.1 copy-start.5
  23.4 0.8 copy-start.18
  92.5 19.2 %collective-permute-start.2 = (bf16[1,6,256,96]{2,3,1,0:T(8,128)(2,1)S(1)}, bf16[1,6,256,96]{2,3,1,0:T(8,128)(2,1)S(1)}, u32[]{:S(2)}, u32[]{:S(2)}) collective-permute-start(bf16[1,6,256,96]{2,3,1,0:T(8,128)(2,1)S(1)} %pad_maximum_fusion.17), channel_id=1, source_target_pairs={{8,0},{12,4},{9,1},{13,5},{10,2},{14,6},{11,3},{15,7},{24,16},{28,... | collective-permute-start | bytes 884744 | tf_op jit(solution)/shard_map/ppermute | solution.py:23
  93.8 18.4 %collective-permute-start.3 = (bf16[1,6,256,96]{2,3,1,0:T(8,128)(2,1)S(1)}, bf16[1,6,256,96]{2,3,1,0:T(8,128)(2,1)S(1)}, u32[]{:S(2)}, u32[]{:S(2)}) collective-permute-start(bf16[1,6,256,96]{2,3,1,0:T(8,128)(2,1)S(1)} %pad_maximum_fusion.17), channel_id=1, source_target_pairs={{4,0},{8,4},{12,8},{5,1},{9,5},{13,9},{6,2},{10,6},{14,10},{7,3},{... | collective-permute-start | bytes 884744 | tf_op jit(solution)/shard_map/ppermute | solution.py:23
  95.6 17.3 %collective-permute-start.6 = (bf16[1,6,256,96]{2,3,1,0:T(8,128)(2,1)S(1)}, bf16[1,6,256,96]{2,3,1,0:T(8,128)(2,1)S(1)}, u32[]{:S(2)}, u32[]{:S(2)}) collective-permute-start(bf16[1,6,256,96]{2,3,1,0:T(8,128)(2,1)S(1)} %pad_maximum_fusion.18), channel_id=1, source_target_pairs={{0,8},{4,12},{1,9},{5,13},{2,10},{6,14},{3,11},{7,15},{16,24},{20,... | collective-permute-start | bytes 884744 | tf_op jit(solution)/shard_map/ppermute | solution.py:23
  101.7 18.6 %collective-permute-start.7 = (bf16[1,6,256,96]{2,3,1,0:T(8,128)(2,1)S(1)}, bf16[1,6,256,96]{2,3,1,0:T(8,128)(2,1)S(1)}, u32[]{:S(2)}, u32[]{:S(2)}) collective-permute-start(bf16[1,6,256,96]{2,3,1,0:T(8,128)(2,1)S(1)} %pad_maximum_fusion.18), channel_id=1, source_target_pairs={{0,4},{4,8},{8,12},{1,5},{5,9},{9,13},{2,6},{6,10},{10,14},{3,7},{... | collective-permute-start | bytes 884744 | tf_op jit(solution)/shard_map/ppermute | solution.py:23
  125.8 1.1 copy-start.3
  126.8 1.3 copy-start.12
  126.8 1.6 copy-start.11
  128.1 0.9 copy-start.10
  128.4 1.1 copy-start.1
  128.4 1.1 copy-start.9
  129.0 1.1 copy-start.2
  129.0 1.1 copy-start.8
  129.5 0.9 copy-start.7
  130.1 0.9 copy-start.13
  130.1 1.0 copy-start.14
  130.1 1.1 copy-start.15
  130.1 1.2 copy-start.17
  130.8 1.1 copy-start.6
  130.8 1.1 copy-start.16
Sparse Core Ops, SparseCore 0:
  127.0 94.7 all-reduce.7
where the time goes:
time: 232 us; the launch traced here: 231 us
  waiting for transfers between devices  88.7 us (38%)
  blocking collectives  59.7 us (26%)
  local copies, waits for them, and re-layouts  30.5 us (13%)
  starting transfers between devices  24.8 us (11%)
  between operations  14.9 us (6%)
  matrix products  7.44 us (3%)
  other arithmetic  5.05 us (2%)
    psum x1, waiting for transfers between devices, on_device(): kernel_total = lax.psum(kernel_local, ('tm', 'space', 'dp'))  88.6 us
    psum x1, blocking collectives, on_device(): sketch_total = lax.psum(sketch_terms, ('tm', 'space', 'dp'))  59.7 us
    unnamed x71, local copies, waits for them, and re-layouts  17.4 us
    ppermute x4, starting transfers between devices, passed_along(): return lax.ppermute(block, axis, route)  12.8 us
    ppermute x2, starting transfers between devices, padded(): before = lax.ppermute(last, axis, up)  9.42 us
  transfers between devices with their start and end apart: 9, of which 1 were waited for; matrix products, arithmetic and copies ran while one was open for 13% of the time, Pallas kernels for 0%

commit v1 on v0

--- a/solution.py
+++ b/solution.py
@@ -21,6 +21,59 @@
     devices = range(lax.axis_size(axis))
     route = [(i - distance, i) for i in devices if i - distance in devices]
     return lax.ppermute(block, axis, route)
+
+
+def exchanged(block, axis, distance):
+    peers = lax.axis_size(axis)
+    return lax.ppermute(block, axis, [(i, i ^ distance) for i in range(peers)])
+
+
+def group_sum(flat, steps):
+    kept = []
+    for axis, distance in steps:
+        upper = (lax.axis_index(axis) // distance) % 2 == 1
+        half = flat.shape[0] // 2
+        low, high = flat[:half], flat[half:]
+        keep = jnp.where(upper, high, low)
+        send = jnp.where(upper, low, high)
+        flat = keep + exchanged(send, axis, distance)
+        kept.append((axis, distance, upper))
+    for axis, distance, upper in reversed(kept):
+        other = exchanged(flat, axis, distance)
+        flat = jnp.where(
+            upper,
+            jnp.concatenate([other, flat]),
+            jnp.concatenate([flat, other]),
+        )
+    return flat
+
+
+def halving_steps():
+    steps = []
+    for axis in ("dp", "space", "tm"):
+        distance = 1
+        while distance < lax.axis_size(axis):
+            steps.append((axis, distance))
+            distance *= 2
+    return steps
+
+
+def reduced_together(kernel_local, sketch_terms):
+    axes = ("tm", "space", "dp")
+    if any(lax.axis_size(a) & (lax.axis_size(a) - 1) for a in axes):
+        return lax.psum(kernel_local, axes), lax.psum(sketch_terms, axes)
+    steps = halving_steps()
+    pieces = 2 ** len(steps)
+    lanes = 128
+    sizes = (kernel_local.size, sketch_terms.size)
+    total = sum(sizes)
+    rows = -(-total // (lanes * pieces)) * pieces
+    flat = jnp.concatenate([kernel_local.reshape(-1), sketch_terms.reshape(-1)])
+    flat = jnp.pad(flat, (0, rows * lanes - total)).reshape(rows, lanes)
+    flat = group_sum(flat, steps).reshape(-1)
+    kernel_total = flat[: sizes[0]].reshape(kernel_local.shape)
+    sketch_total = flat[sizes[0] : total].reshape(sketch_terms.shape)
+    return kernel_total, sketch_total
 
 
 def silu_slope(value):
@@ -92,8 +145,7 @@
         * lax.axis_size("space")
         * lax.axis_size("dp")
     )
-    sketch_total = lax.psum(sketch_terms, ("tm", "space", "dp"))
-    kernel_total = lax.psum(kernel_local, ("tm", "space", "dp"))
+    kernel_total, sketch_total = reduced_together(kernel_local, sketch_terms)
     sketches = sketch_total / jnp.float32(total_pixels)
     weight_grad = kernel_total * (1.0 / jnp.sqrt(jnp.float32(total_pixels)))
     return (input_grad, weight_grad, sketches)

time: 232 us -> 115 us (0.50)
  waiting for transfers between devices: 88.7 us -> 25.7 us
  blocking collectives: 59.7 us -> 0 us
  starting transfers between devices: 24.8 us -> 38.2 us
  between operations: 14.9 us -> 1.69 us
  local copies, waits for them, and re-layouts: 30.5 us -> 36.9 us
    psum x1 -> x0, waiting for transfers between devices: 88.6 us -> none  [on_device(): kernel_total = lax.psum(kernel_local, ('tm', 'space', 'dp'))]
    psum x1 -> x0, blocking collectives: 59.7 us -> none  [on_device(): sketch_total = lax.psum(sketch_terms, ('tm', 'space', 'dp'))]
    ppermute x0 -> x8, waiting for transfers between devices: none -> 25.7 us  [exchanged(): return lax.ppermute(block, axis, [(i, i ^ distance) for i in range(peers)])]
    ppermute x0 -> x8, starting transfers between devices: none -> 12.4 us  [exchanged(): return lax.ppermute(block, axis, [(i, i ^ distance) for i in range(peers)])]
    slice x5, local copies, waits for them, and re-layouts: 1.63 us -> 4.96 us  [on_device(): source[:, 2 - b:2 - b + rows, 2 - e:2 - e + width, :]]
    mul x1, other arithmetic: 2.48 us -> 0.07 us  [on_device(): weight_grad = kernel_total * (1.0 / jnp.sqrt(jnp.float32(total_pixels)))]
    unnamed x71 -> x74, local copies, waits for them, and re-layouts: 17.4 us -> 15.4 us
  transfers between devices with their start and end apart: 9 -> 16, of which waited for: 1 -> 6; matrix products, arithmetic and copies ran while one was open for 13% -> 36% of each run, Pallas kernels for 0% -> 0%
where the time goes in v1:
time: 115 us; the launch traced here: 114 us
  starting transfers between devices  38.2 us (33%)
  local copies, waits for them, and re-layouts  36.9 us (32%)
  waiting for transfers between devices  25.7 us (22%)
  matrix products  6.48 us (6%)
  other arithmetic  5.03 us (4%)
  between operations  1.69 us (1%)
    ppermute x8, waiting for transfers between devices, exchanged(): return lax.ppermute(block, axis, [(i, i ^ distance) for i in range(peers)])  25.7 us
    unnamed x74, local copies, waits for them, and re-layouts  15.4 us
    ppermute x4, starting transfers between devices, passed_along(): return lax.ppermute(block, axis, route)  13.7 us
    ppermute x8, starting transfers between devices, exchanged(): return lax.ppermute(block, axis, [(i, i ^ distance) for i in range(peers)])  12.4 us
    ppermute x2, starting transfers between devices, padded(): before = lax.ppermute(last, axis, up)  9.42 us
    slice x5, local copies, waits for them, and re-layouts, on_device(): source[:, 2 - b:2 - b + rows, 2 - e:2 - e + width, :]  4.96 us
    concatenate x9, local copies, waits for them, and re-layouts, on_device(): jnp.concatenate([source[:, 2 - b:2 - b + rows, 2 - e:2 - e + width, :] fo...  4.91 us
    concatenate x8, local copies, waits for them, and re-layouts, on_device(): jnp.concatenate([earlier[:, b:b + rows, e:e + width, :] for e in range(3)...  3.67 us
  transfers between devices with their start and end apart: 16, of which 6 were waited for; matrix products, arithmetic and copies ran while one was open for 36% of the time, Pallas kernels for 0%

profile of v1, /device:TPU:0, one launch (start us, length us, event | category | flops | bytes accessed | tf_op | source)
XLA Modules:
  0.0 114.0 jit_solution(6480640907763155540)
XLA Ops:
  0.7 0.9 fusion.36
  1.5 1.3 %collective-permute-start.1 = (bf16[1,1,256,96]{2,3,1,0:T(8,128)(2,1)S(1)}, bf16[1,1,256,96]{2,3,1,0:T(8,128)(2,1)S(1)}, u32[]{:S(2)}, u32[]{:S(2)}) collective-permute-start(bf16[1,1,256,96]{2,3,1,0:T(8,128)(2,1)S(1)} %get-tuple-element.73), channel_id=1, source_target_pairs={{2,0},{3,1},{6,4},{7,5},{10,8},{11,9},{14,12},{15,13},{18,16},{19,... | collective-permute-start | bytes 147464 | tf_op jit(solution)/shard_map/ppermute | solution.py:15
  2.8 4.9 %collective-permute-start = (bf16[1,1,256,96]{2,3,1,0:T(8,128)(2,1)S(1)}, bf16[1,1,256,96]{2,3,1,0:T(8,128)(2,1)S(1)}, u32[]{:S(2)}, u32[]{:S(2)}) collective-permute-start(bf16[1,1,256,96]{2,3,1,0:T(8,128)(2,1)S(1)} %get-tuple-element.72), channel_id=1, source_target_pairs={{0,2},{1,3},{4,6},{5,7},{8,10},{9,11},{12,14},{13,15},{16,18},{17,... | collective-permute-start | bytes 147464 | tf_op jit(solution)/shard_map/ppermute | solution.py:14
  7.7 1.0 fusion.29
  8.8 1.3 %collective-permute-start.5 = (bf16[1,1,256,96]{2,3,1,0:T(8,128)(2,1)S(1)}, bf16[1,1,256,96]{2,3,1,0:T(8,128)(2,1)S(1)}, u32[]{:S(2)}, u32[]{:S(2)}) collective-permute-start(bf16[1,1,256,96]{2,3,1,0:T(8,128)(2,1)S(1)} %get-tuple-element.69), channel_id=1, source_target_pairs={{2,0},{3,1},{6,4},{7,5},{10,8},{11,9},{14,12},{15,13},{18,16},{19,... | collective-permute-start | bytes 147464 | tf_op jit(solution)/shard_map/ppermute | solution.py:15
  10.1 4.5 %collective-permute-start.4 = (bf16[1,1,256,96]{2,3,1,0:T(8,128)(2,1)S(1)}, bf16[1,1,256,96]{2,3,1,0:T(8,128)(2,1)S(1)}, u32[]{:S(2)}, u32[]{:S(2)}) collective-permute-start(bf16[1,1,256,96]{2,3,1,0:T(8,128)(2,1)S(1)} %get-tuple-element.68), channel_id=1, source_target_pairs={{0,2},{1,3},{4,6},{5,7},{8,10},{9,11},{12,14},{13,15},{16,18},{17,... | collective-permute-start | bytes 147464 | tf_op jit(solution)/shard_map/ppermute | solution.py:14
  14.6 1.1 copy.31
  16.3 0.6 copy-done.7
  17.1 0.5 copy-done.19
  18.2 0.7 copy.45
  18.9 0.7 copy.46
  19.7 0.7 copy.47
  20.4 0.7 copy.48
  21.5 0.7 copy.52
  22.4 0.7 copy.62
  23.1 0.7 copy.53
  23.9 0.7 reshape.267
  24.6 0.8 pad_maximum_fusion.17
  25.4 1.3 %collective-permute-start.2 = (bf16[1,6,256,96]{2,3,1,0:T(8,128)(2,1)}, bf16[1,6,256,96]{2,3,1,0:T(8,128)(2,1)S(1)}, u32[]{:S(2)}, u32[]{:S(2)}) collective-permute-start(bf16[1,6,256,96]{2,3,1,0:T(8,128)(2,1)} %pad_maximum_fusion.17), channel_id=1, source_target_pairs={{8,0},{12,4},{9,1},{13,5},{10,2},{14,6},{11,3},{15,7},{24,16},{28,... | collective-permute-start | bytes 884744 | tf_op jit(solution)/shard_map/ppermute | solution.py:23
  26.6 1.3 %collective-permute-start.3 = (bf16[1,6,256,96]{2,3,1,0:T(8,128)(2,1)}, bf16[1,6,256,96]{2,3,1,0:T(8,128)(2,1)}, u32[]{:S(2)}, u32[]{:S(2)}) collective-permute-start(bf16[1,6,256,96]{2,3,1,0:T(8,128)(2,1)} %pad_maximum_fusion.17), channel_id=1, source_target_pairs={{4,0},{8,4},{12,8},{5,1},{9,5},{13,9},{6,2},{10,6},{14,10},{7,3},{... | collective-permute-start | bytes 884744 | tf_op jit(solution)/shard_map/ppermute | solution.py:23
  27.9 1.8 %pad_slice_fusion.19 = (bf16[1,4,256,96]{2,3,1,0:T(8,128)(2,1)S(1)}, bf16[1,4,256,96]{2,3,1,0:T(8,128)(2,1)S(1)}, bf16[1,4,256,96]{2,3,1,0:T(8,128)(2,1)S(1)}, b...) fusion(bf16[1,6,256,96]{2,3,1,0:T(8,128)(2,1)} %pad_maximum_fusion.17), kind=kLoop, calls=%fused_computation.83 | loop fusion | bytes 1474560 | tf_op jit(solution)/shard_map/slice | solution.py:116
  29.8 6.7 %collective-permute-start.6 = (bf16[1,6,256,96]{2,3,1,0:T(8,128)(2,1)S(1)}, bf16[1,6,256,96]{2,3,1,0:T(8,128)(2,1)S(1)}, u32[]{:S(2)}, u32[]{:S(2)}) collective-permute-start(bf16[1,6,256,96]{2,3,1,0:T(8,128)(2,1)S(1)} %pad_maximum_fusion.18), channel_id=1, source_target_pairs={{0,8},{4,12},{1,9},{5,13},{2,10},{6,14},{3,11},{7,15},{16,24},{20,... | collective-permute-start | bytes 884744 | tf_op jit(solution)/shard_map/ppermute | solution.py:23
  36.5 4.4 %collective-permute-start.7 = (bf16[1,6,256,96]{2,3,1,0:T(8,128)(2,1)S(1)}, bf16[1,6,256,96]{2,3,1,0:T(8,128)(2,1)S(1)}, u32[]{:S(2)}, u32[]{:S(2)}) collective-permute-start(bf16[1,6,256,96]{2,3,1,0:T(8,128)(2,1)S(1)} %pad_maximum_fusion.18), channel_id=1, source_target_pairs={{0,4},{4,8},{8,12},{1,5},{5,9},{9,13},{2,6},{6,10},{10,14},{3,7},{... | collective-permute-start | bytes 884744 | tf_op jit(solution)/shard_map/ppermute | solution.py:23
  41.9 0.9 copy.60
  43.0 0.7 copy.63
  43.9 0.7 copy.61
  45.1 0.9 copy.64
  55.6 1.1 pad_maximum_fusion.4
  56.7 0.9 pad_maximum_fusion.6
  57.6 0.8 slice.345
  58.4 1.0 reshape_reshape.3
  59.4 1.6 %copy.11 = bf16[1,4,256,288]{2,1,3,0:T(4,128)(2,1)S(1)} copy(bf16[1,4,256,288]{2,3,1,0:T(8,128)(2,1)} %get-tuple-element.74) | data formatting | bytes 1179648 | tf_op jit(solution)/shard_map/concatenate | solution.py:115
  63.1 2.4 %pad_slice_fusion.25 = (bf16[1,4,256,96]{2,3,1,0:T(8,128)(2,1)S(1)}, bf16[1,4,256,96]{2,3,1,0:T(8,128)(2,1)S(1)}, bf16[1,4,256,96]{2,3,1,0:T(8,128)(2,1)S(1)}, b...) fusion(bf16[1,6,256,96]{2,3,1,0:T(8,128)(2,1)} %collective-perm, ...), kind=kLoop, calls=%fused_computation.89 | loop fusion | bytes 2654208 | tf_op jit(solution)/shard_map/slice | solution.py:116
  67.5 0.7 copy-done.10
  68.5 7.6 %collective-permute-done.9 = f32[500,128]{1,0:T(8,128)S(1)} collective-permute-done((f32[500,128]{1,0:T(8,128)S(1)}, f32[500,128]{1,0:T(8,128)S(1)}, u32[]{:S(2)}, u32[]{:S(2)}) %collective-permute-start.9) | collective-permute-done | bytes 256032 | tf_op jit(solution)/shard_map/ppermute | solution.py:28
  76.2 5.6 %collective-permute-start.10 = (f32[250,128]{1,0:T(8,128)S(1)}, f32[250,128]{1,0:T(8,128)S(1)}, u32[]{:S(2)}, u32[]{:S(2)}) collective-permute-start(f32[250,128]{1,0:T(8,128)S(1)} %slice_select_fusion.2), channel_id=1, source_target_pairs={{0,4},{4,0},{8,12},{12,8},{1,5},{5,1},{9,13},{13,9},{2,6},{6,2},{1... | collective-permute-start | bytes 384008 | tf_op jit(solution)/shard_map/ppermute | solution.py:28
  82.7 2.4 %collective-permute-done.10 = f32[250,128]{1,0:T(8,128)S(1)} collective-permute-done((f32[250,128]{1,0:T(8,128)S(1)}, f32[250,128]{1,0:T(8,128)S(1)}, u32[]{:S(2)}, u32[]{:S(2)}) %collective-permute-start.10) | collective-permute-done | bytes 128032 | tf_op jit(solution)/shard_map/ppermute | solution.py:28
  85.1 3.7 %collective-permute-start.11 = (f32[125,128]{1,0:T(8,128)S(1)}, f32[125,128]{1,0:T(8,128)S(1)}, u32[]{:S(2)}, u32[]{:S(2)}) collective-permute-start(f32[125,128]{1,0:T(8,128)S(1)} %slice_select_fusion.3), channel_id=1, source_target_pairs={{0,8},{4,12},{8,0},{12,4},{1,9},{5,13},{9,1},{13,5},{2,10},{6,14},... | collective-permute-start | bytes 192008 | tf_op jit(solution)/shard_map/ppermute | solution.py:28
  89.1 2.6 %collective-permute-done.11 = f32[125,128]{1,0:T(8,128)S(1)} collective-permute-done((f32[125,128]{1,0:T(8,128)S(1)}, f32[125,128]{1,0:T(8,128)S(1)}, u32[]{:S(2)}, u32[]{:S(2)}) %collective-permute-start.11) | collective-permute-done | bytes 64032 | tf_op jit(solution)/shard_map/ppermute | solution.py:28
  91.8 2.3 %collective-permute-start.12 = (f32[125,128]{1,0:T(8,128)S(1)}, f32[125,128]{1,0:T(8,128)S(1)}, u32[]{:S(2)}, u32[]{:S(2)}) collective-permute-start(f32[125,128]{1,0:T(8,128)S(1)} %select_add_fusion.3), channel_id=1, source_target_pairs={{0,8},{4,12},{8,0},{12,4},{1,9},{5,13},{9,1},{13,5},{2,10},{6,14},... | collective-permute-start | bytes 192008 | tf_op jit(solution)/shard_map/ppermute | solution.py:28
  94.7 3.0 %collective-permute-done.12 = f32[125,128]{1,0:T(8,128)S(1)} collective-permute-done((f32[125,128]{1,0:T(8,128)S(1)}, f32[125,128]{1,0:T(8,128)S(1)}, u32[]{:S(2)}, u32[]{:S(2)}) %collective-permute-start.12) | collective-permute-done | bytes 64032 | tf_op jit(solution)/shard_map/ppermute | solution.py:28
  98.1 4.6 %collective-permute-done.13 = f32[250,128]{1,0:T(8,128)S(1)} collective-permute-done((f32[250,128]{1,0:T(8,128)S(1)}, f32[250,128]{1,0:T(8,128)S(1)}, u32[]{:S(2)}, u32[]{:S(2)}) %collective-permute-start.13) | collective-permute-done | bytes 128032 | tf_op jit(solution)/shard_map/ppermute | solution.py:28
  102.7 0.6 collective-permute-start.14
  103.7 5.5 %collective-permute-done.14 = f32[500,128]{1,0:T(8,128)S(1)} collective-permute-done((f32[500,128]{1,0:T(8,128)S(1)}, f32[500,128]{1,0:T(8,128)S(1)}, u32[]{:S(2)}, u32[]{:S(2)}) %collective-permute-start.14) | collective-permute-done | bytes 256032 | tf_op jit(solution)/shard_map/ppermute | solution.py:28
  109.7 0.5 copy-done.5
  110.9 0.7 copy.43
  111.8 1.4 %mul.53 = f32[3,3,3,96,96]{4,3,2,1,0:T(8,128)} reshape(f32[1944,128]{1,0:T(8,128)S(1)} %slice_multiply_fusion) | data formatting | bytes 1990656 | tf_op jit(solution)/shard_map/mul | solution.py:150
  113.2 0.7 copy.44
  (149 shorter events, 21.2 us)
Async XLA Ops:
  0.6 15.1 %copy-start = (bf16[1,1,4,256,96]{3,4,2,1,0:T(8,128)(2,1)S(1)}, bf16[1,1,4,256,96]{3,4,2,1,0:T(8,128)(2,1)}, u32[]{:S(2)}) copy-start(bf16[1,1,4,256,96]{3,4,2,1,0:T(8,128)(2,1)} %param.5) | copy-start | bytes 589828
  0.6 15.3 %copy-start.6 = (bf16[1,1,4,256,96]{3,4,2,1,0:T(8,128)(2,1)S(1)}, bf16[1,1,4,256,96]{3,4,2,1,0:T(8,128)(2,1)}, u32[]{:S(2)}) copy-start(bf16[1,1,4,256,96]{3,4,2,1,0:T(8,128)(2,1)} %param.4) | copy-start | bytes 589828
  1.5 23.1 %collective-permute-start.1 = (bf16[1,1,256,96]{2,3,1,0:T(8,128)(2,1)S(1)}, bf16[1,1,256,96]{2,3,1,0:T(8,128)(2,1)S(1)}, u32[]{:S(2)}, u32[]{:S(2)}) collective-permute-start(bf16[1,1,256,96]{2,3,1,0:T(8,128)(2,1)S(1)} %get-tuple-element.73), channel_id=1, source_target_pairs={{2,0},{3,1},{6,4},{7,5},{10,8},{11,9},{14,12},{15,13},{18,16},{19,... | collective-permute-start | bytes 147464 | tf_op jit(solution)/shard_map/ppermute | solution.py:15
  2.8 21.8 %collective-permute-start = (bf16[1,1,256,96]{2,3,1,0:T(8,128)(2,1)S(1)}, bf16[1,1,256,96]{2,3,1,0:T(8,128)(2,1)S(1)}, u32[]{:S(2)}, u32[]{:S(2)}) collective-permute-start(bf16[1,1,256,96]{2,3,1,0:T(8,128)(2,1)S(1)} %get-tuple-element.72), channel_id=1, source_target_pairs={{0,2},{1,3},{4,6},{5,7},{8,10},{9,11},{12,14},{13,15},{16,18},{17,... | collective-permute-start | bytes 147464 | tf_op jit(solution)/shard_map/ppermute | solution.py:14
  8.8 21.0 %collective-permute-start.5 = (bf16[1,1,256,96]{2,3,1,0:T(8,128)(2,1)S(1)}, bf16[1,1,256,96]{2,3,1,0:T(8,128)(2,1)S(1)}, u32[]{:S(2)}, u32[]{:S(2)}) collective-permute-start(bf16[1,1,256,96]{2,3,1,0:T(8,128)(2,1)S(1)} %get-tuple-element.69), channel_id=1, source_target_pairs={{2,0},{3,1},{6,4},{7,5},{10,8},{11,9},{14,12},{15,13},{18,16},{19,... | collective-permute-start | bytes 147464 | tf_op jit(solution)/shard_map/ppermute | solution.py:15
  10.1 19.7 %collective-permute-start.4 = (bf16[1,1,256,96]{2,3,1,0:T(8,128)(2,1)S(1)}, bf16[1,1,256,96]{2,3,1,0:T(8,128)(2,1)S(1)}, u32[]{:S(2)}, u32[]{:S(2)}) collective-permute-start(bf16[1,1,256,96]{2,3,1,0:T(8,128)(2,1)S(1)} %get-tuple-element.68), channel_id=1, source_target_pairs={{0,2},{1,3},{4,6},{5,7},{8,10},{9,11},{12,14},{13,15},{16,18},{17,... | collective-permute-start | bytes 147464 | tf_op jit(solution)/shard_map/ppermute | solution.py:14
  15.7 1.1 copy-start.7
  16.8 0.8 copy-start.19
  16.9 1.0 copy-start.4
  25.4 29.8 %collective-permute-start.2 = (bf16[1,6,256,96]{2,3,1,0:T(8,128)(2,1)}, bf16[1,6,256,96]{2,3,1,0:T(8,128)(2,1)S(1)}, u32[]{:S(2)}, u32[]{:S(2)}) collective-permute-start(bf16[1,6,256,96]{2,3,1,0:T(8,128)(2,1)} %pad_maximum_fusion.17), channel_id=1, source_target_pairs={{8,0},{12,4},{9,1},{13,5},{10,2},{14,6},{11,3},{15,7},{24,16},{28,... | collective-permute-start | bytes 884744 | tf_op jit(solution)/shard_map/ppermute | solution.py:23
  26.6 36.4 %collective-permute-start.3 = (bf16[1,6,256,96]{2,3,1,0:T(8,128)(2,1)}, bf16[1,6,256,96]{2,3,1,0:T(8,128)(2,1)}, u32[]{:S(2)}, u32[]{:S(2)}) collective-permute-start(bf16[1,6,256,96]{2,3,1,0:T(8,128)(2,1)} %pad_maximum_fusion.17), channel_id=1, source_target_pairs={{4,0},{8,4},{12,8},{5,1},{9,5},{13,9},{6,2},{10,6},{14,10},{7,3},{... | collective-permute-start | bytes 884744 | tf_op jit(solution)/shard_map/ppermute | solution.py:23
  29.8 17.9 %collective-permute-start.6 = (bf16[1,6,256,96]{2,3,1,0:T(8,128)(2,1)S(1)}, bf16[1,6,256,96]{2,3,1,0:T(8,128)(2,1)S(1)}, u32[]{:S(2)}, u32[]{:S(2)}) collective-permute-start(bf16[1,6,256,96]{2,3,1,0:T(8,128)(2,1)S(1)} %pad_maximum_fusion.18), channel_id=1, source_target_pairs={{0,8},{4,12},{1,9},{5,13},{2,10},{6,14},{3,11},{7,15},{16,24},{20,... | collective-permute-start | bytes 884744 | tf_op jit(solution)/shard_map/ppermute | solution.py:23
  36.5 13.5 %collective-permute-start.7 = (bf16[1,6,256,96]{2,3,1,0:T(8,128)(2,1)S(1)}, bf16[1,6,256,96]{2,3,1,0:T(8,128)(2,1)S(1)}, u32[]{:S(2)}, u32[]{:S(2)}) collective-permute-start(bf16[1,6,256,96]{2,3,1,0:T(8,128)(2,1)S(1)} %pad_maximum_fusion.18), channel_id=1, source_target_pairs={{0,4},{4,8},{8,12},{1,5},{5,9},{9,13},{2,6},{6,10},{10,14},{3,7},{... | collective-permute-start | bytes 884744 | tf_op jit(solution)/shard_map/ppermute | solution.py:23
  59.4 1.7 %copy-start.3 = (bf16[1,4,256,288]{2,3,1,0:T(8,128)(2,1)S(1)}, bf16[1,4,256,288]{2,3,1,0:T(8,128)(2,1)}, u32[]{:S(2)}) copy-start(bf16[1,4,256,288]{2,3,1,0:T(8,128)(2,1)} %get-tuple-element.75) | copy-start | bytes 1769476
  61.1 1.1 copy-start.2
  62.2 0.7 copy-start.13
  63.0 4.3 %collective-permute-start.8 = (f32[1000,128]{1,0:T(8,128)S(1)}, f32[1000,128]{1,0:T(8,128)S(1)}, u32[]{:S(2)}, u32[]{:S(2)}) collective-permute-start(f32[1000,128]{1,0:T(8,128)S(1)} %slice_select_fusion), channel_id=1, source_target_pairs={{0,1},{1,0},{2,3},{3,2},{4,5},{5,4},{6,7},{7,6},{8,9},{9,8},{10,11... | collective-permute-start | bytes 1536008 | tf_op jit(solution)/shard_map/ppermute | solution.py:28
  65.6 0.9 copy-start.12
  66.1 0.9 copy-start.11
  67.3 0.9 copy-start.10
  67.4 8.7 %collective-permute-start.9 = (f32[500,128]{1,0:T(8,128)S(1)}, f32[500,128]{1,0:T(8,128)S(1)}, u32[]{:S(2)}, u32[]{:S(2)}) collective-permute-start(f32[500,128]{1,0:T(8,128)S(1)} %slice_select_fusion.1), channel_id=1, source_target_pairs={{0,2},{2,0},{1,3},{3,1},{4,6},{6,4},{5,7},{7,5},{8,10},{10,8},{9,1... | collective-permute-start | bytes 768008 | tf_op jit(solution)/shard_map/ppermute | solution.py:28
  68.2 13.6 %copy-start.9 = (bf16[1,1,3,96,96]{3,4,2,1,0:T(8,128)(2,1)S(1)}, bf16[1,1,3,96,96]{3,4,2,1,0:T(8,128)(2,1)}, u32[]{:S(2)}) copy-start(bf16[1,1,3,96,96]{3,4,2,1,0:T(8,128)(2,1)} %copy.48) | copy-start | bytes 165892
  76.2 8.9 %collective-permute-start.10 = (f32[250,128]{1,0:T(8,128)S(1)}, f32[250,128]{1,0:T(8,128)S(1)}, u32[]{:S(2)}, u32[]{:S(2)}) collective-permute-start(f32[250,128]{1,0:T(8,128)S(1)} %slice_select_fusion.2), channel_id=1, source_target_pairs={{0,4},{4,0},{8,12},{12,8},{1,5},{5,1},{9,13},{13,9},{2,6},{6,2},{1... | collective-permute-start | bytes 384008 | tf_op jit(solution)/shard_map/ppermute | solution.py:28
  85.1 6.7 %collective-permute-start.11 = (f32[125,128]{1,0:T(8,128)S(1)}, f32[125,128]{1,0:T(8,128)S(1)}, u32[]{:S(2)}, u32[]{:S(2)}) collective-permute-start(f32[125,128]{1,0:T(8,128)S(1)} %slice_select_fusion.3), channel_id=1, source_target_pairs={{0,8},{4,12},{8,0},{12,4},{1,9},{5,13},{9,1},{13,5},{2,10},{6,14},... | collective-permute-start | bytes 192008 | tf_op jit(solution)/shard_map/ppermute | solution.py:28
  91.8 5.9 %collective-permute-start.12 = (f32[125,128]{1,0:T(8,128)S(1)}, f32[125,128]{1,0:T(8,128)S(1)}, u32[]{:S(2)}, u32[]{:S(2)}) collective-permute-start(f32[125,128]{1,0:T(8,128)S(1)} %select_add_fusion.3), channel_id=1, source_target_pairs={{0,8},{4,12},{8,0},{12,4},{1,9},{5,13},{9,1},{13,5},{2,10},{6,14},... | collective-permute-start | bytes 192008 | tf_op jit(solution)/shard_map/ppermute | solution.py:28
  94.7 8.7 %copy-start.1 = (bf16[36,8,4,256]{3,1,2,0:T(8,128)(2,1)S(1)}, bf16[36,8,4,256]{3,1,2,0:T(8,128)(2,1)}, u32[]{:S(2)}) copy-start(bf16[36,8,4,256]{3,1,2,0:T(8,128)(2,1)} %copy.60) | copy-start | bytes 1769476
  97.7 5.0 %collective-permute-start.13 = (f32[250,128]{1,0:T(8,128)S(1)}, f32[250,128]{1,0:T(8,128)S(1)}, u32[]{:S(2)}, u32[]{:S(2)}) collective-permute-start(f32[250,128]{1,0:T(8,128)S(1)} %maximum_select_fusion.3), channel_id=1, source_target_pairs={{0,4},{4,0},{8,12},{12,8},{1,5},{5,1},{9,13},{13,9},{2,6},{6,2},{1... | collective-permute-start | bytes 384008 | tf_op jit(solution)/shard_map/ppermute | solution.py:28
  102.7 6.4 %collective-permute-start.14 = (f32[500,128]{1,0:T(8,128)S(1)}, f32[500,128]{1,0:T(8,128)S(1)}, u32[]{:S(2)}, u32[]{:S(2)}) collective-permute-start(f32[500,128]{1,0:T(8,128)S(1)} %maximum_select_fusion.2), channel_id=1, source_target_pairs={{0,2},{2,0},{1,3},{3,1},{4,6},{6,4},{5,7},{7,5},{8,10},{10,8},{9,1... | collective-permute-start | bytes 768008 | tf_op jit(solution)/shard_map/ppermute | solution.py:28
  103.3 6.0 %copy-start.14 = (bf16[12,8,4,256]{3,1,2,0:T(8,128)(2,1)S(1)}, bf16[12,8,4,256]{3,1,2,0:T(8,128)(2,1)}, u32[]{:S(2)}) copy-start(bf16[12,8,4,256]{3,1,2,0:T(8,128)(2,1)} %copy.62) | copy-start | bytes 589828
  103.3 6.0 %copy-start.15 = (bf16[12,8,4,256]{3,1,2,0:T(8,128)(2,1)S(1)}, bf16[12,8,4,256]{3,1,2,0:T(8,128)(2,1)}, u32[]{:S(2)}) copy-start(bf16[12,8,4,256]{3,1,2,0:T(8,128)(2,1)} %copy.63) | copy-start | bytes 589828
  103.3 6.0 %copy-start.16 = (bf16[12,8,4,256]{3,1,2,0:T(8,128)(2,1)S(1)}, bf16[12,8,4,256]{3,1,2,0:T(8,128)(2,1)}, u32[]{:S(2)}) copy-start(bf16[12,8,4,256]{3,1,2,0:T(8,128)(2,1)} %copy.61) | copy-start | bytes 589828
  103.3 6.0 %copy-start.18 = (bf16[1,1,3,96,96]{3,4,2,1,0:T(8,128)(2,1)S(1)}, bf16[1,1,3,96,96]{3,4,2,1,0:T(8,128)(2,1)}, u32[]{:S(2)}) copy-start(bf16[1,1,3,96,96]{3,4,2,1,0:T(8,128)(2,1)} %copy.52) | copy-start | bytes 165892
  109.2 1.0 copy-start.5
  109.2 1.2 %copy-start.8 = (bf16[36,8,4,256]{3,1,2,0:T(8,128)(2,1)S(1)}, bf16[36,8,4,256]{3,1,2,0:T(8,128)(2,1)}, u32[]{:S(2)}) copy-start(bf16[36,8,4,256]{3,1,2,0:T(8,128)(2,1)} %copy.64) | copy-start | bytes 1769476
  109.2 1.2 %copy-start.17 = (bf16[1,1,3,96,96]{3,4,2,1,0:T(8,128)(2,1)S(1)}, bf16[1,1,3,96,96]{3,4,2,1,0:T(8,128)(2,1)}, u32[]{:S(2)}) copy-start(bf16[1,1,3,96,96]{3,4,2,1,0:T(8,128)(2,1)} %copy.53) | copy-start | bytes 165892
  109.2 2.4 %collective-permute-start.15 = (f32[1000,128]{1,0:T(8,128)S(1)}, f32[1000,128]{1,0:T(8,128)S(1)}, u32[]{:S(2)}, u32[]{:S(2)}) collective-permute-start(f32[1000,128]{1,0:T(8,128)S(1)} %maximum_select_fusion.1), channel_id=1, source_target_pairs={{0,1},{1,0},{2,3},{3,2},{4,5},{5,4},{6,7},{7,6},{8,9},{9,8},{10,11... | collective-permute-start | bytes 1536008 | tf_op jit(solution)/shard_map/ppermute | solution.py:28

commit v2 on v1

--- a/solution.py
+++ b/solution.py
@@ -103,10 +103,6 @@
     grad_frames = [pad_columns(grad_rows)]
     for lag in (1, 2):
         grad_frames.append(pad_columns(passed_along(grad_rows, "tm", -lag)))
-    hid_rows = padded(hidden, (("space", 1),), 1)
-    hid_frames = [pad_columns(hid_rows)]
-    for lag in (1, 2):
-        hid_frames.append(pad_columns(passed_along(hid_rows, "tm", lag)))
     grad_hidden = jnp.zeros((count, chans), jnp.float32)
     kernel_terms = []
     for a in range(3):
@@ -120,11 +116,8 @@
             grad_hidden = grad_hidden + jnp.dot(
                 slab, weight_mat, preferred_element_type=jnp.float32
             )
-            earlier = hid_frames[2 - a]
-            hid_slab = jnp.concatenate(
-                [earlier[:, b : b + rows, e : e + width, :] for e in range(3)], axis=-1
-            ).reshape(count, 3 * chans)
-            kernel_terms.append(contract_rows(hid_slab, grad_flat).reshape(3, chans, chans))
+            term = contract_rows(hid_flat, slab).reshape(chans, 3, chans)
+            kernel_terms.append(jnp.transpose(term, (1, 0, 2)))
     kernel_local = jnp.stack(kernel_terms).reshape(3, 3, 3, chans, chans)
     xflat = xin.reshape(count, chans).astype(jnp.float32)
     input_grad = (grad_hidden * silu_slope(xflat)).astype(jnp.bfloat16)

time: 115 us -> 103 us (0.90)
  starting transfers between devices: 38.2 us -> 13.2 us
  waiting for transfers between devices: 25.7 us -> 50 us
  local copies, waits for them, and re-layouts: 36.9 us -> 24 us
  matrix products: 6.48 us -> 7.83 us
    ppermute x4 -> x2, waiting for transfers between devices: 0.01 us -> 19 us  [passed_along(): return lax.ppermute(block, axis, route)]
    ppermute x4 -> x2, starting transfers between devices: 13.7 us -> 2.58 us  [passed_along(): return lax.ppermute(block, axis, route)]
    ppermute x8, starting transfers between devices: 12.4 us -> 4.47 us  [exchanged(): return lax.ppermute(block, axis, [(i, i ^ distance) for i in range(peers)])]
    ppermute x8, waiting for transfers between devices: 25.7 us -> 30.7 us  [exchanged(): return lax.ppermute(block, axis, [(i, i ^ distance) for i in range(peers)])]
    ppermute x2 -> x1, starting transfers between devices: 9.42 us -> 4.87 us  [padded(): before = lax.ppermute(last, axis, up)]
    concatenate x8 -> x0, local copies, waits for them, and re-layouts: 3.67 us -> none  [on_device(): jnp.concatenate([earlier[:, b:b + rows, e:e + width, :] for e in range(3)...]
    slice x5, local copies, waits for them, and re-layouts: 4.96 us -> 1.6 us  [on_device(): source[:, 2 - b:2 - b + rows, 2 - e:2 - e + width, :]]
    unnamed x74 -> x64, local copies, waits for them, and re-layouts: 15.4 us -> 12.3 us
  transfers between devices with their start and end apart: 16 -> 12, of which waited for: 6 -> 9; matrix products, arithmetic and copies ran while one was open for 36% -> 22% of each run, Pallas kernels for 0% -> 0%
where the time goes in v2:
time: 103 us; the launch traced here: 102 us
  waiting for transfers between devices  50 us (49%)
  local copies, waits for them, and re-layouts  24 us (23%)
  starting transfers between devices  13.2 us (13%)
  matrix products  7.83 us (8%)
  other arithmetic  5.73 us (6%)
  between operations  1.6 us (2%)
    ppermute x8, waiting for transfers between devices, exchanged(): return lax.ppermute(block, axis, [(i, i ^ distance) for i in range(peers)])  30.7 us
    ppermute x2, waiting for transfers between devices, passed_along(): return lax.ppermute(block, axis, route)  19 us
    unnamed x64, local copies, waits for them, and re-layouts  12.3 us
    ppermute x1, starting transfers between devices, padded(): before = lax.ppermute(last, axis, up)  4.87 us
    ppermute x8, starting transfers between devices, exchanged(): return lax.ppermute(block, axis, [(i, i ^ distance) for i in range(peers)])  4.47 us
    dot_general x11, matrix products, contract_rows(): lax.dot_general(left, right, (((0,), (0,)), ((), ())), preferred_element_...  4.44 us
    concatenate x9, local copies, waits for them, and re-layouts, on_device(): jnp.concatenate([source[:, 2 - b:2 - b + rows, 2 - e:2 - e + width, :] fo...  3.68 us
    dot_general x9, matrix products, on_device(): jnp.dot(slab, weight_mat, preferred_element_type=jnp.float32)  3.01 us
  transfers between devices with their start and end apart: 12, of which 9 were waited for; matrix products, arithmetic and copies ran while one was open for 22% of the time, Pallas kernels for 0%

profile of v2, /device:TPU:0, one launch (start us, length us, event | category | flops | bytes accessed | tf_op | source)
XLA Modules:
  0.0 102.4 jit_solution(11720201502041338764)
XLA Ops:
  0.6 0.9 fusion.20
  1.5 4.9 %collective-permute-start = (bf16[1,1,256,96]{2,3,1,0:T(8,128)(2,1)S(1)}, bf16[1,1,256,96]{2,3,1,0:T(8,128)(2,1)S(1)}, u32[]{:S(2)}, u32[]{:S(2)}) collective-permute-start(bf16[1,1,256,96]{2,3,1,0:T(8,128)(2,1)S(1)} %get-tuple-element.44), channel_id=1, source_target_pairs={{0,2},{1,3},{4,6},{5,7},{8,10},{9,11},{12,14},{13,15},{16,18},{17,... | collective-permute-start | bytes 147464 | tf_op jit(solution)/shard_map/ppermute | solution.py:14
  6.4 1.3 %collective-permute-start.1 = (bf16[1,1,256,96]{2,3,1,0:T(8,128)(2,1)S(1)}, bf16[1,1,256,96]{2,3,1,0:T(8,128)(2,1)S(1)}, u32[]{:S(2)}, u32[]{:S(2)}) collective-permute-start(bf16[1,1,256,96]{2,3,1,0:T(8,128)(2,1)S(1)} %get-tuple-element.45), channel_id=1, source_target_pairs={{2,0},{3,1},{6,4},{7,5},{10,8},{11,9},{14,12},{15,13},{18,16},{19,... | collective-permute-start | bytes 147464 | tf_op jit(solution)/shard_map/ppermute | solution.py:15
  7.7 1.3 %convolution_bitcast_fusion.9 = f32[96,96]{1,0:T(8,128)S(1)} fusion(bf16[1,1,4,256,96]{3,4,2,1,0:T(8,128)(2,1)} %param.5), kind=kOutput, calls=%fused_computation.28 | convolution fusion | flops 18874368 | bytes 233472 | tf_op jit(solution)/shard_map/dot_general | solution.py:89
  9.0 0.8 add_convert_fusion
  9.7 1.0 %multiply_convert_fusion = bf16[1,1,4,256,96]{3,4,2,1,0:T(8,128)(2,1)S(1)} fusion(bf16[1,1,4,256,96]{3,4,2,1,0:T(8,128)(2,1)} %param.4), kind=kLoop, calls=%fused_computation.72 | loop fusion | flops 589824 | bytes 393216 | tf_op jit(solution)/shard_map/convert_element_type | solution.py:99
  12.4 1.3 %collective-permute-start.3 = (bf16[1,6,256,96]{2,3,1,0:T(8,128)(2,1)S(1)}, bf16[1,6,256,96]{2,3,1,0:T(8,128)(2,1)S(1)}, u32[]{:S(2)}, u32[]{:S(2)}) collective-permute-start(bf16[1,6,256,96]{2,3,1,0:T(8,128)(2,1)S(1)} %pad_maximum_fusion.8), channel_id=1, source_target_pairs={{4,0},{8,4},{12,8},{5,1},{9,5},{13,9},{6,2},{10,6},{14,10},{7,3},{... | collective-permute-start | bytes 884744 | tf_op jit(solution)/shard_map/ppermute | solution.py:23
  13.7 1.3 %collective-permute-start.2 = (bf16[1,6,256,96]{2,3,1,0:T(8,128)(2,1)S(1)}, bf16[1,6,256,96]{2,3,1,0:T(8,128)(2,1)S(1)}, u32[]{:S(2)}, u32[]{:S(2)}) collective-permute-start(bf16[1,6,256,96]{2,3,1,0:T(8,128)(2,1)S(1)} %pad_maximum_fusion.8), channel_id=1, source_target_pairs={{8,0},{12,4},{9,1},{13,5},{10,2},{14,6},{11,3},{15,7},{24,16},{28,... | collective-permute-start | bytes 884744 | tf_op jit(solution)/shard_map/ppermute | solution.py:23
  15.0 0.4 pad_slice_fusion.1
  15.9 0.5 copy.27
  16.5 0.5 copy.21
  17.1 19.0 %collective-permute-done.2 = bf16[1,6,256,96]{2,3,1,0:T(8,128)(2,1)S(1)} collective-permute-done((bf16[1,6,256,96]{2,3,1,0:T(8,128)(2,1)S(1)}, bf16[1,6,256,96]{2,3,1,0:T(8,128)(2,1)S(1)}, u32[]{:S(2)}, u32[]{:S(2)}) %collective-permute-start.2) | collective-permute-done | bytes 294944 | tf_op jit(solution)/shard_map/ppermute | solution.py:23
  36.2 0.4 pad_slice_fusion.13
  36.7 0.5 copy.13
  37.3 0.5 copy.9
  37.9 0.5 copy.11
  38.5 0.4 pad_slice_fusion.7
  39.0 0.5 copy.19
  39.7 0.5 copy.15
  40.3 0.5 copy.17
  44.0 1.8 %slice.221 = f32[1944,128]{1,0:T(8,128)} reshape(f32[9,3,96,96]{3,2,1,0:T(8,128)S(1)} %fusion.2) | data formatting | bytes 1990656 | tf_op jit(solution)/shard_map/slice | solution.py:36
  45.7 0.8 reshape_reshape.3
  46.5 1.9 %slice_select_fusion = f32[1000,128]{1,0:T(8,128)} fusion(f32[1944,128]{1,0:T(8,128)} %slice.221, pred[]{:T(512)S(6)} %eq.17, f32[6144]{0:T(1024)S(1)} %reshape.166, f32[248832]{0:T(1024)S(1)} %reshape_reshape.3), kind=kLoop, calls=%fused_computation.71 | loop fusion | flops 768000 | bytes 2043905 | tf_op jit(solution)/shard_map/jit(_where)/select_n | solution.py:38
  48.7 0.8 copy.54
  49.6 0.8 fusion.19
  50.4 1.0 copy.42
  51.4 1.0 copy.41
  52.4 1.0 copy.40
  53.4 1.0 copy.39
  54.4 1.0 copy.38
  55.3 1.0 copy.37
  56.3 1.0 copy.36
  57.3 1.0 copy.35
  58.8 0.9 copy-done.10
  59.7 1.2 %select_add_fusion = f32[1000,128]{1,0:T(8,128)S(1)} fusion(f32[1000,128]{1,0:T(8,128)} %collective-permute-done.4, f32[1944,128]{1,0:T(8,128)S(1)} %copy-done.10, pred[]{:T(512)S(6)} %eq.17, f32[6144]{0:T(1024)S(1)} %reshape.166, f32[248832]{0:T(1024)S(1)} %reshape_reshape.3), kind=kLoop, calls=%fused_computation.70 | loop fusion | flops 896000 | bytes 2555905 | tf_op jit(solution)/shard_map/add | solution.py:39
  60.9 2.4 %collective-permute-start.5 = (f32[500,128]{1,0:T(8,128)S(1)}, f32[500,128]{1,0:T(8,128)S(1)}, u32[]{:S(2)}, u32[]{:S(2)}) collective-permute-start(f32[500,128]{1,0:T(8,128)S(1)} %slice_select_fusion.1), channel_id=1, source_target_pairs={{0,2},{2,0},{1,3},{3,1},{4,6},{6,4},{5,7},{7,5},{8,10},{10,8},{9,1... | collective-permute-start | bytes 768008 | tf_op jit(solution)/shard_map/ppermute | solution.py:28
  63.6 6.5 %collective-permute-done.5 = f32[500,128]{1,0:T(8,128)S(1)} collective-permute-done((f32[500,128]{1,0:T(8,128)S(1)}, f32[500,128]{1,0:T(8,128)S(1)}, u32[]{:S(2)}, u32[]{:S(2)}) %collective-permute-start.5) | collective-permute-done | bytes 256032 | tf_op jit(solution)/shard_map/ppermute | solution.py:28
  70.3 0.5 convolution_add_fusion.6
  70.8 4.8 %collective-permute-done.6 = f32[250,128]{1,0:T(8,128)S(1)} collective-permute-done((f32[250,128]{1,0:T(8,128)S(1)}, f32[250,128]{1,0:T(8,128)S(1)}, u32[]{:S(2)}, u32[]{:S(2)}) %collective-permute-start.6) | collective-permute-done | bytes 128032 | tf_op jit(solution)/shard_map/ppermute | solution.py:28
  76.0 5.2 %collective-permute-done.7 = f32[125,128]{1,0:T(8,128)S(1)} collective-permute-done((f32[125,128]{1,0:T(8,128)S(1)}, f32[125,128]{1,0:T(8,128)S(1)}, u32[]{:S(2)}, u32[]{:S(2)}) %collective-permute-start.7) | collective-permute-done | bytes 64032 | tf_op jit(solution)/shard_map/ppermute | solution.py:28
  81.7 4.9 %collective-permute-done.8 = f32[125,128]{1,0:T(8,128)S(1)} collective-permute-done((f32[125,128]{1,0:T(8,128)S(1)}, f32[125,128]{1,0:T(8,128)S(1)}, u32[]{:S(2)}, u32[]{:S(2)}) %collective-permute-start.8) | collective-permute-done | bytes 64032 | tf_op jit(solution)/shard_map/ppermute | solution.py:28
  87.0 4.6 %collective-permute-done.9 = f32[250,128]{1,0:T(8,128)S(1)} collective-permute-done((f32[250,128]{1,0:T(8,128)S(1)}, f32[250,128]{1,0:T(8,128)S(1)}, u32[]{:S(2)}, u32[]{:S(2)}) %collective-permute-start.9) | collective-permute-done | bytes 128032 | tf_op jit(solution)/shard_map/ppermute | solution.py:28
  91.7 1.7 %collective-permute-start.10 = (f32[500,128]{1,0:T(8,128)S(1)}, f32[500,128]{1,0:T(8,128)S(1)}, u32[]{:S(2)}, u32[]{:S(2)}) collective-permute-start(f32[500,128]{1,0:T(8,128)S(1)} %maximum_select_fusion.2), channel_id=1, source_target_pairs={{0,2},{2,0},{1,3},{3,1},{4,6},{6,4},{5,7},{7,5},{8,10},{10,8},{9,1... | collective-permute-start | bytes 768008 | tf_op jit(solution)/shard_map/ppermute | solution.py:28
  93.7 4.4 %collective-permute-done.10 = f32[500,128]{1,0:T(8,128)S(1)} collective-permute-done((f32[500,128]{1,0:T(8,128)S(1)}, f32[500,128]{1,0:T(8,128)S(1)}, u32[]{:S(2)}, u32[]{:S(2)}) %collective-permute-start.10) | collective-permute-done | bytes 256032 | tf_op jit(solution)/shard_map/ppermute | solution.py:28
  98.5 0.4 fusion.1
  99.0 0.7 copy.32
  100.3 0.7 copy.33
  101.0 1.4 %mul.50 = f32[3,3,3,96,96]{4,3,2,1,0:T(8,128)} reshape(f32[1944,128]{1,0:T(8,128)S(1)} %slice_multiply_fusion) | data formatting | bytes 1990656 | tf_op jit(solution)/shard_map/mul | solution.py:143
  (111 shorter events, 10.0 us)
Async XLA Ops:
  0.6 10.9 %copy-start.11 = (bf16[1,1,4,256,96]{3,4,2,1,0:T(8,128)(2,1)S(1)}, bf16[1,1,4,256,96]{3,4,2,1,0:T(8,128)(2,1)}, u32[]{:S(2)}) copy-start(bf16[1,1,4,256,96]{3,4,2,1,0:T(8,128)(2,1)} %param.5) | copy-start | bytes 589828
  1.5 10.6 %collective-permute-start = (bf16[1,1,256,96]{2,3,1,0:T(8,128)(2,1)S(1)}, bf16[1,1,256,96]{2,3,1,0:T(8,128)(2,1)S(1)}, u32[]{:S(2)}, u32[]{:S(2)}) collective-permute-start(bf16[1,1,256,96]{2,3,1,0:T(8,128)(2,1)S(1)} %get-tuple-element.44), channel_id=1, source_target_pairs={{0,2},{1,3},{4,6},{5,7},{8,10},{9,11},{12,14},{13,15},{16,18},{17,... | collective-permute-start | bytes 147464 | tf_op jit(solution)/shard_map/ppermute | solution.py:14
  6.4 6.0 %collective-permute-start.1 = (bf16[1,1,256,96]{2,3,1,0:T(8,128)(2,1)S(1)}, bf16[1,1,256,96]{2,3,1,0:T(8,128)(2,1)S(1)}, u32[]{:S(2)}, u32[]{:S(2)}) collective-permute-start(bf16[1,1,256,96]{2,3,1,0:T(8,128)(2,1)S(1)} %get-tuple-element.45), channel_id=1, source_target_pairs={{2,0},{3,1},{6,4},{7,5},{10,8},{11,9},{14,12},{15,13},{18,16},{19,... | collective-permute-start | bytes 147464 | tf_op jit(solution)/shard_map/ppermute | solution.py:15
  12.4 26.1 %collective-permute-start.3 = (bf16[1,6,256,96]{2,3,1,0:T(8,128)(2,1)S(1)}, bf16[1,6,256,96]{2,3,1,0:T(8,128)(2,1)S(1)}, u32[]{:S(2)}, u32[]{:S(2)}) collective-permute-start(bf16[1,6,256,96]{2,3,1,0:T(8,128)(2,1)S(1)} %pad_maximum_fusion.8), channel_id=1, source_target_pairs={{4,0},{8,4},{12,8},{5,1},{9,5},{13,9},{6,2},{10,6},{14,10},{7,3},{... | collective-permute-start | bytes 884744 | tf_op jit(solution)/shard_map/ppermute | solution.py:23
  13.7 22.5 %collective-permute-start.2 = (bf16[1,6,256,96]{2,3,1,0:T(8,128)(2,1)S(1)}, bf16[1,6,256,96]{2,3,1,0:T(8,128)(2,1)S(1)}, u32[]{:S(2)}, u32[]{:S(2)}) collective-permute-start(bf16[1,6,256,96]{2,3,1,0:T(8,128)(2,1)S(1)} %pad_maximum_fusion.8), channel_id=1, source_target_pairs={{8,0},{12,4},{9,1},{13,5},{10,2},{14,6},{11,3},{15,7},{24,16},{28,... | collective-permute-start | bytes 884744 | tf_op jit(solution)/shard_map/ppermute | solution.py:23
  16.5 27.1 %copy-start.14 = (bf16[36,8,4,256]{3,1,2,0:T(8,128)(2,1)}, bf16[36,8,4,256]{3,1,2,0:T(8,128)(2,1)S(1)}, u32[]{:S(2)}) copy-start(bf16[36,8,4,256]{3,1,2,0:T(8,128)(2,1)S(1)} %copy.53) | copy-start | bytes 1769476
  17.1 26.1 %copy-start.12 = (bf16[1024,288]{0,1:T(8,128)(2,1)}, bf16[1024,288]{0,1:T(8,128)(2,1)S(1)}, u32[]{:S(2)}) copy-start(bf16[1024,288]{0,1:T(8,128)(2,1)S(1)} %constant_dynamic-update-slice_fusion) | copy-start | bytes 1769476
  37.3 4.3 %copy-start = (bf16[36,8,4,256]{3,1,2,0:T(8,128)(2,1)}, bf16[36,8,4,256]{3,1,2,0:T(8,128)(2,1)S(1)}, u32[]{:S(2)}) copy-start(bf16[36,8,4,256]{3,1,2,0:T(8,128)(2,1)S(1)} %copy.45) | copy-start | bytes 1769476
  37.9 2.9 %copy-start.8 = (bf16[36,8,4,256]{3,1,2,0:T(8,128)(2,1)}, bf16[36,8,4,256]{3,1,2,0:T(8,128)(2,1)S(1)}, u32[]{:S(2)}) copy-start(bf16[36,8,4,256]{3,1,2,0:T(8,128)(2,1)S(1)} %copy.43) | copy-start | bytes 1769476
  38.5 2.7 %copy-start.4 = (bf16[36,8,4,256]{3,1,2,0:T(8,128)(2,1)}, bf16[36,8,4,256]{3,1,2,0:T(8,128)(2,1)S(1)}, u32[]{:S(2)}) copy-start(bf16[36,8,4,256]{3,1,2,0:T(8,128)(2,1)S(1)} %copy.44) | copy-start | bytes 1769476
  40.3 1.7 %copy-start.6 = (bf16[36,8,4,256]{3,1,2,0:T(8,128)(2,1)}, bf16[36,8,4,256]{3,1,2,0:T(8,128)(2,1)S(1)}, u32[]{:S(2)}) copy-start(bf16[36,8,4,256]{3,1,2,0:T(8,128)(2,1)S(1)} %copy.46) | copy-start | bytes 1769476
  40.8 1.4 %copy-start.2 = (bf16[36,8,4,256]{3,1,2,0:T(8,128)(2,1)}, bf16[36,8,4,256]{3,1,2,0:T(8,128)(2,1)S(1)}, u32[]{:S(2)}) copy-start(bf16[36,8,4,256]{3,1,2,0:T(8,128)(2,1)S(1)} %copy.47) | copy-start | bytes 1769476
  46.5 2.0 %copy-start.16 = (bf16[1,1,4,256,96]{3,4,2,1,0:T(8,128)(2,1)S(1)}, bf16[1,1,4,256,96]{3,4,2,1,0:T(8,128)(2,1)}, u32[]{:S(2)}) copy-start(bf16[1,1,4,256,96]{3,4,2,1,0:T(8,128)(2,1)} %param.4) | copy-start | bytes 589828
  48.5 1.1 %copy-start.17 = (bf16[3,3,3,96,96]{4,3,2,1,0:T(8,128)(2,1)S(1)}, bf16[3,3,3,96,96]{4,3,2,1,0:T(8,128)(2,1)}, u32[]{:S(2)}) copy-start(bf16[3,3,3,96,96]{4,3,2,1,0:T(8,128)(2,1)} %param.6) | copy-start | bytes 1492996
  48.5 10.3 %collective-permute-start.4 = (f32[1000,128]{1,0:T(8,128)}, f32[1000,128]{1,0:T(8,128)}, u32[]{:S(2)}, u32[]{:S(2)}) collective-permute-start(f32[1000,128]{1,0:T(8,128)} %slice_select_fusion), channel_id=1, source_target_pairs={{0,1},{1,0},{2,3},{3,2},{4,5},{5,4},{6,7},{7,6},{8,9},{9,8},{10,11... | collective-permute-start | bytes 1536008 | tf_op jit(solution)/shard_map/ppermute | solution.py:28
  49.6 8.9 %copy-start.9 = (bf16[36,8,4,256]{3,1,2,0:T(8,128)(2,1)S(1)}, bf16[36,8,4,256]{3,1,2,0:T(8,128)(2,1)}, u32[]{:S(2)}) copy-start(bf16[36,8,4,256]{3,1,2,0:T(8,128)(2,1)} %copy-done.8) | copy-start | bytes 1769476
  58.5 1.2 %copy-start.10 = (f32[1944,128]{1,0:T(8,128)S(1)}, f32[1944,128]{1,0:T(8,128)}, u32[]{:S(2)}) copy-start(f32[1944,128]{1,0:T(8,128)} %slice.221) | copy-start | bytes 2985988
  58.8 4.5 %copy-start.5 = (bf16[36,8,4,256]{3,1,2,0:T(8,128)(2,1)S(1)}, bf16[36,8,4,256]{3,1,2,0:T(8,128)(2,1)}, u32[]{:S(2)}) copy-start(bf16[36,8,4,256]{3,1,2,0:T(8,128)(2,1)} %copy-done.4) | copy-start | bytes 1769476
  60.9 9.2 %collective-permute-start.5 = (f32[500,128]{1,0:T(8,128)S(1)}, f32[500,128]{1,0:T(8,128)S(1)}, u32[]{:S(2)}, u32[]{:S(2)}) collective-permute-start(f32[500,128]{1,0:T(8,128)S(1)} %slice_select_fusion.1), channel_id=1, source_target_pairs={{0,2},{2,0},{1,3},{3,1},{4,6},{6,4},{5,7},{7,5},{8,10},{10,8},{9,1... | collective-permute-start | bytes 768008 | tf_op jit(solution)/shard_map/ppermute | solution.py:28
  63.3 7.0 %copy-start.1 = (bf16[36,8,4,256]{3,1,2,0:T(8,128)(2,1)S(1)}, bf16[36,8,4,256]{3,1,2,0:T(8,128)(2,1)}, u32[]{:S(2)}) copy-start(bf16[36,8,4,256]{3,1,2,0:T(8,128)(2,1)} %copy-done) | copy-start | bytes 1769476
  70.2 5.5 %copy-start.7 = (bf16[36,8,4,256]{3,1,2,0:T(8,128)(2,1)S(1)}, bf16[36,8,4,256]{3,1,2,0:T(8,128)(2,1)}, u32[]{:S(2)}) copy-start(bf16[36,8,4,256]{3,1,2,0:T(8,128)(2,1)} %copy-done.6) | copy-start | bytes 1769476
  70.2 5.3 %collective-permute-start.6 = (f32[250,128]{1,0:T(8,128)S(1)}, f32[250,128]{1,0:T(8,128)S(1)}, u32[]{:S(2)}, u32[]{:S(2)}) collective-permute-start(f32[250,128]{1,0:T(8,128)S(1)} %slice_select_fusion.2), channel_id=1, source_target_pairs={{0,4},{4,0},{8,12},{12,8},{1,5},{5,1},{9,13},{13,9},{2,6},{6,2},{1... | collective-permute-start | bytes 384008 | tf_op jit(solution)/shard_map/ppermute | solution.py:28
  70.8 10.6 %copy-start.3 = (bf16[36,8,4,256]{3,1,2,0:T(8,128)(2,1)S(1)}, bf16[36,8,4,256]{3,1,2,0:T(8,128)(2,1)}, u32[]{:S(2)}) copy-start(bf16[36,8,4,256]{3,1,2,0:T(8,128)(2,1)} %copy-done.2) | copy-start | bytes 1769476
  75.6 5.7 %collective-permute-start.7 = (f32[125,128]{1,0:T(8,128)S(1)}, f32[125,128]{1,0:T(8,128)S(1)}, u32[]{:S(2)}, u32[]{:S(2)}) collective-permute-start(f32[125,128]{1,0:T(8,128)S(1)} %slice_select_fusion.3), channel_id=1, source_target_pairs={{0,8},{4,12},{8,0},{12,4},{1,9},{5,13},{9,1},{13,5},{2,10},{6,14},... | collective-permute-start | bytes 192008 | tf_op jit(solution)/shard_map/ppermute | solution.py:28
  81.3 5.3 %collective-permute-start.8 = (f32[125,128]{1,0:T(8,128)S(1)}, f32[125,128]{1,0:T(8,128)S(1)}, u32[]{:S(2)}, u32[]{:S(2)}) collective-permute-start(f32[125,128]{1,0:T(8,128)S(1)} %select_add_fusion.3), channel_id=1, source_target_pairs={{0,8},{4,12},{8,0},{12,4},{1,9},{5,13},{9,1},{13,5},{2,10},{6,14},... | collective-permute-start | bytes 192008 | tf_op jit(solution)/shard_map/ppermute | solution.py:28
  86.6 5.0 %collective-permute-start.9 = (f32[250,128]{1,0:T(8,128)S(1)}, f32[250,128]{1,0:T(8,128)S(1)}, u32[]{:S(2)}, u32[]{:S(2)}) collective-permute-start(f32[250,128]{1,0:T(8,128)S(1)} %maximum_select_fusion.3), channel_id=1, source_target_pairs={{0,4},{4,0},{8,12},{12,8},{1,5},{5,1},{9,13},{13,9},{2,6},{6,2},{1... | collective-permute-start | bytes 384008 | tf_op jit(solution)/shard_map/ppermute | solution.py:28
  91.7 6.4 %collective-permute-start.10 = (f32[500,128]{1,0:T(8,128)S(1)}, f32[500,128]{1,0:T(8,128)S(1)}, u32[]{:S(2)}, u32[]{:S(2)}) collective-permute-start(f32[500,128]{1,0:T(8,128)S(1)} %maximum_select_fusion.2), channel_id=1, source_target_pairs={{0,2},{2,0},{1,3},{3,1},{4,6},{6,4},{5,7},{7,5},{8,10},{10,8},{9,1... | collective-permute-start | bytes 768008 | tf_op jit(solution)/shard_map/ppermute | solution.py:28
  93.3 4.8 %copy-start.13 = (bf16[1024,288]{0,1:T(8,128)(2,1)S(1)}, bf16[1024,288]{0,1:T(8,128)(2,1)}, u32[]{:S(2)}) copy-start(bf16[1024,288]{0,1:T(8,128)(2,1)} %copy-done.12) | copy-start | bytes 1769476
  93.7 4.9 %copy-start.15 = (bf16[36,8,4,256]{3,1,2,0:T(8,128)(2,1)S(1)}, bf16[36,8,4,256]{3,1,2,0:T(8,128)(2,1)}, u32[]{:S(2)}) copy-start(bf16[36,8,4,256]{3,1,2,0:T(8,128)(2,1)} %copy-done.14) | copy-start | bytes 1769476
  93.7 4.9 %copy-start.18 = (f32[12,8,4,256]{3,1,2,0:T(8,128)S(1)}, f32[12,8,4,256]{3,1,2,0:T(8,128)}, u32[]{:S(2)}) copy-start(f32[12,8,4,256]{3,1,2,0:T(8,128)} %copy.54) | copy-start | bytes 1179652
  98.1 2.0 %collective-permute-start.11 = (f32[1000,128]{1,0:T(8,128)S(1)}, f32[1000,128]{1,0:T(8,128)S(1)}, u32[]{:S(2)}, u32[]{:S(2)}) collective-permute-start(f32[1000,128]{1,0:T(8,128)S(1)} %maximum_select_fusion.1), channel_id=1, source_target_pairs={{0,1},{1,0},{2,3},{3,2},{4,5},{5,4},{6,7},{7,6},{8,9},{9,8},{10,11... | collective-permute-start | bytes 1536008 | tf_op jit(solution)/shard_map/ppermute | solution.py:28

commit v3 on v2

--- a/solution.py
+++ b/solution.py
@@ -76,6 +76,27 @@
     return kernel_total, sketch_total
 
 
+def from_neighbour(block, frames_ahead, rows_ahead):
+    frames, rows = lax.axis_size("tm"), lax.axis_size("space")
+    route = []
+    for t in range(frames):
+        for r in range(rows):
+            source = (t + frames_ahead, r + rows_ahead)
+            if 0 <= source[0] < frames and 0 <= source[1] < rows:
+                route.append((source[0] * rows + source[1], t * rows + r))
+    return lax.ppermute(block, ("tm", "space"), route)
+
+
+def cotangent_frames(grad_out):
+    result = []
+    for ahead in range(3):
+        centre = grad_out if ahead == 0 else from_neighbour(grad_out, ahead, 0)
+        above = from_neighbour(grad_out[:, -1:], ahead, -1)
+        below = from_neighbour(grad_out[:, :1], ahead, 1)
+        result.append(pad_columns(jnp.concatenate([above, centre, below], axis=1)))
+    return result
+
+
 def silu_slope(value):
     sig = jax.nn.sigmoid(value)
     return sig * (1.0 + value * (1.0 - sig))
@@ -99,11 +120,9 @@
     hidden = jax.nn.silu(xin.astype(jnp.float32)).astype(jnp.bfloat16)
     hid_flat = hidden.reshape(count, chans)
     grad_flat = grad_out.reshape(count, chans)
-    grad_rows = padded(grad_out, (("space", 1),), 1)
-    grad_frames = [pad_columns(grad_rows)]
-    for lag in (1, 2):
-        grad_frames.append(pad_columns(passed_along(grad_rows, "tm", -lag)))
+    grad_frames = cotangent_frames(grad_out)
     grad_hidden = jnp.zeros((count, chans), jnp.float32)
+    flipped = jnp.swapaxes(conv_weight, 3, 4)
     kernel_terms = []
     for a in range(3):
         for b in range(3):
@@ -112,9 +131,8 @@
                 [source[:, 2 - b : 2 - b + rows, 2 - e : 2 - e + width, :] for e in range(3)],
                 axis=-1,
             ).reshape(count, 3 * chans)
-            weight_mat = jnp.transpose(conv_weight[a, b], (0, 2, 1)).reshape(3 * chans, chans)
             grad_hidden = grad_hidden + jnp.dot(
-                slab, weight_mat, preferred_element_type=jnp.float32
+                slab, flipped[a, b].reshape(3 * chans, chans), preferred_element_type=jnp.float32
             )
             term = contract_rows(hid_flat, slab).reshape(chans, 3, chans)
             kernel_terms.append(jnp.transpose(term, (1, 0, 2)))

time: 103 us -> 90.4 us (0.88)
  waiting for transfers between devices: 50 us -> 32.2 us
  starting transfers between devices: 13.2 us -> 24.2 us
  local copies, waits for them, and re-layouts: 24 us -> 17.9 us
    ppermute x4 -> x8, waiting for transfers between devices: 19.3 us -> 4.82 us  [from_neighbour(): return lax.ppermute(block, ('tm', 'space'), route)]
    ppermute x8, starting transfers between devices: 4.47 us -> 10.6 us  [exchanged(): return lax.ppermute(block, axis, [(i, i ^ distance) for i in range(peers)])]
    unnamed x64 -> x54, local copies, waits for them, and re-layouts: 12.3 us -> 6.62 us
    ppermute x4 -> x8, starting transfers between devices: 8.74 us -> 13.6 us  [from_neighbour(): return lax.ppermute(block, ('tm', 'space'), route)]
    ppermute x8, waiting for transfers between devices: 30.7 us -> 27.4 us  [exchanged(): return lax.ppermute(block, axis, [(i, i ^ distance) for i in range(peers)])]
  transfers between devices with their start and end apart: 12 -> 16, of which waited for: 9 -> 8; matrix products, arithmetic and copies ran while one was open for 22% -> 19% of each run, Pallas kernels for 0% -> 0%
where the time goes in v3:
time: 90.4 us; the launch traced here: 89.9 us
  waiting for transfers between devices  32.2 us (36%)
  starting transfers between devices  24.2 us (27%)
  local copies, waits for them, and re-layouts  17.9 us (20%)
  matrix products  7.64 us (8%)
  other arithmetic  6.41 us (7%)
  between operations  1.55 us (2%)
    ppermute x8, waiting for transfers between devices, exchanged(): return lax.ppermute(block, axis, [(i, i ^ distance) for i in range(peers)])  27.4 us
    ppermute x8, starting transfers between devices, from_neighbour(): return lax.ppermute(block, ('tm', 'space'), route)  13.6 us
    ppermute x8, starting transfers between devices, exchanged(): return lax.ppermute(block, axis, [(i, i ^ distance) for i in range(peers)])  10.6 us
    unnamed x54, local copies, waits for them, and re-layouts  6.62 us
    ppermute x8, waiting for transfers between devices, from_neighbour(): return lax.ppermute(block, ('tm', 'space'), route)  4.82 us
    dot_general x11, matrix products, contract_rows(): lax.dot_general(left, right, (((0,), (0,)), ((), ())), preferred_element_...  4.41 us
    concatenate x9, local copies, waits for them, and re-layouts, on_device(): jnp.concatenate([source[:, 2 - b:2 - b + rows, 2 - e:2 - e + width, :] fo...  3.68 us
    dot_general x9, matrix products, on_device(): jnp.dot(slab, flipped[a, b].reshape(3 * chans, chans), preferred_element_...  2.86 us
  transfers between devices with their start and end apart: 16, of which 8 were waited for; matrix products, arithmetic and copies ran while one was open for 19% of the time, Pallas kernels for 0%

profile of v3, /device:TPU:0, one launch (start us, length us, event | category | flops | bytes accessed | tf_op | source)
XLA Modules:
  0.0 89.9 jit_solution(9158137041044619273)
XLA Ops:
  0.6 1.4 %collective-permute-start.1 = (bf16[1,4,256,96]{2,3,1,0:T(8,128)(2,1)}, bf16[1,4,256,96]{2,3,1,0:T(8,128)(2,1)S(1)}, u32[]{:S(2)}, u32[]{:S(2)}) collective-permute-start(bf16[1,4,256,96]{2,3,1,0:T(8,128)(2,1)} %bitcast.246), channel_id=1, source_target_pairs={{8,0},{10,2},{12,4},{14,6},{9,1},{11,3},{13,5},{15,7},{24,16},{26,... | collective-permute-start | bytes 589832 | tf_op jit(solution)/shard_map/ppermute | solution.py:87
  2.1 0.8 fusion.32
  2.9 0.7 collective-permute-start
  3.6 5.5 %collective-permute-start.6 = (bf16[1,1,256,96]{2,3,1,0:T(8,128)(2,1)S(1)}, bf16[1,1,256,96]{2,3,1,0:T(8,128)(2,1)S(1)}, u32[]{:S(2)}, u32[]{:S(2)}) collective-permute-start(bf16[1,1,256,96]{2,3,1,0:T(8,128)(2,1)S(1)} %get-tuple-element.44), channel_id=1, source_target_pairs={{0,2},{4,6},{8,10},{12,14},{1,3},{5,7},{9,11},{13,15},{16,18},{20,... | collective-permute-start | bytes 147464 | tf_op jit(solution)/shard_map/ppermute | solution.py:87
  9.1 1.3 %collective-permute-start.2 = (bf16[1,1,256,96]{2,3,1,0:T(8,128)(2,1)S(1)}, bf16[1,1,256,96]{2,3,1,0:T(8,128)(2,1)S(1)}, u32[]{:S(2)}, u32[]{:S(2)}) collective-permute-start(bf16[1,1,256,96]{2,3,1,0:T(8,128)(2,1)S(1)} %get-tuple-element.45), channel_id=1, source_target_pairs={{10,0},{14,4},{11,1},{15,5},{26,16},{30,20},{27,17},{31,21}} | collective-permute-start | bytes 147464 | tf_op jit(solution)/shard_map/ppermute | solution.py:87
  10.4 1.3 %collective-permute-start.7 = (bf16[1,1,256,96]{2,3,1,0:T(8,128)(2,1)S(1)}, bf16[1,1,256,96]{2,3,1,0:T(8,128)(2,1)S(1)}, u32[]{:S(2)}, u32[]{:S(2)}) collective-permute-start(bf16[1,1,256,96]{2,3,1,0:T(8,128)(2,1)S(1)} %get-tuple-element.45), channel_id=1, source_target_pairs={{2,0},{6,4},{10,8},{14,12},{3,1},{7,5},{11,9},{15,13},{18,16},{22,... | collective-permute-start | bytes 147464 | tf_op jit(solution)/shard_map/ppermute | solution.py:87
  11.7 1.3 %convolution_bitcast_fusion.9 = f32[96,96]{1,0:T(8,128)S(1)} fusion(bf16[1,1,4,256,96]{3,4,2,1,0:T(8,128)(2,1)} %param.5), kind=kOutput, calls=%fused_computation.30 | convolution fusion | flops 18874368 | bytes 233472 | tf_op jit(solution)/shard_map/dot_general | solution.py:110
  12.9 1.0 %multiply_convert_fusion = bf16[1,1,4,256,96]{3,4,2,1,0:T(8,128)(2,1)S(1)} fusion(bf16[1,1,4,256,96]{3,4,2,1,0:T(8,128)(2,1)} %param.4), kind=kLoop, calls=%fused_computation.71 | loop fusion | flops 589824 | bytes 393216 | tf_op jit(solution)/shard_map/convert_element_type | solution.py:120
  14.0 0.8 add_convert_fusion
  16.1 1.3 %collective-permute-start.4 = (bf16[1,4,256,96]{2,3,1,0:T(8,128)(2,1)S(1)}, bf16[1,4,256,96]{2,3,1,0:T(8,128)(2,1)S(1)}, u32[]{:S(2)}, u32[]{:S(2)}) collective-permute-start(bf16[1,4,256,96]{2,3,1,0:T(8,128)(2,1)S(1)} %bitcast.248), channel_id=1, source_target_pairs={{4,0},{6,2},{8,4},{10,6},{12,8},{14,10},{5,1},{7,3},{9,5},{11,7},{... | collective-permute-start | bytes 589832 | tf_op jit(solution)/shard_map/ppermute | solution.py:87
  17.4 0.7 collective-permute-start.3
  19.1 0.5 copy.16
  19.7 0.5 copy.20
  20.3 1.5 %collective-permute-start.5 = (bf16[1,1,256,96]{2,3,1,0:T(8,128)(2,1)S(1)}, bf16[1,1,256,96]{2,3,1,0:T(8,128)(2,1)S(1)}, u32[]{:S(2)}, u32[]{:S(2)}) collective-permute-start(bf16[1,1,256,96]{2,3,1,0:T(8,128)(2,1)S(1)} %get-tuple-element.45), channel_id=1, source_target_pairs={{6,0},{10,4},{14,8},{7,1},{11,5},{15,9},{22,16},{26,20},{30,24},{2... | collective-permute-start | bytes 147464 | tf_op jit(solution)/shard_map/ppermute | solution.py:87
  22.5 0.5 copy.9
  23.0 0.5 copy.11
  23.6 0.5 copy.12
  24.2 4.8 %collective-permute-done.5 = bf16[1,1,256,96]{2,3,1,0:T(8,128)(2,1)S(1)} collective-permute-done((bf16[1,1,256,96]{2,3,1,0:T(8,128)(2,1)S(1)}, bf16[1,1,256,96]{2,3,1,0:T(8,128)(2,1)S(1)}, u32[]{:S(2)}, u32[]{:S(2)}) %collective-permute-start.5) | collective-permute-done | bytes 49184 | tf_op jit(solution)/shard_map/ppermute | solution.py:87
  29.7 0.5 copy.13
  30.3 0.5 copy.14
  30.9 0.5 copy.15
  31.4 0.3 fusion.10
  31.8 0.3 fusion.9
  33.5 0.3 fusion.4
  33.8 0.3 fusion.3
  34.2 0.3 fusion.2
  34.5 1.8 %slice.223 = f32[1944,128]{1,0:T(8,128)} reshape(f32[9,3,96,96]{3,2,1,0:T(8,128)S(1)} %fusion.2) | data formatting | bytes 1990656 | tf_op jit(solution)/shard_map/slice | solution.py:36
  36.3 0.8 reshape_reshape.3
  37.1 1.9 %slice_select_fusion = f32[1000,128]{1,0:T(8,128)} fusion(f32[1944,128]{1,0:T(8,128)} %slice.223, pred[]{:T(512)S(6)} %eq.17, f32[6144]{0:T(1024)S(1)} %reshape.130, f32[248832]{0:T(1024)S(1)} %reshape_reshape.3), kind=kLoop, calls=%fused_computation.64 | loop fusion | flops 768000 | bytes 2043905 | tf_op jit(solution)/shard_map/jit(_where)/select_n | solution.py:38
  39.0 0.9 %copy.21 = f32[1,1,4,256,96]{3,2,4,1,0:T(4,128)} copy(bf16[1,1,4,256,96]{3,4,2,1,0:T(8,128)(2,1)S(1)} %copy-done.16) | data formatting | bytes 589824 | tf_op jit(solution)/shard_map/convert_element_type | solution.py:140
  40.0 1.4 %copy.10 = bf16[3,3,3,96,96]{3,4,2,1,0:T(8,128)(2,1)S(1)} copy(bf16[3,3,3,96,96]{4,3,2,1,0:T(8,128)(2,1)} %param.6) | data formatting | bytes 995328 | tf_op args[2]
  41.4 1.9 %copy.37 = f32[12,8,4,256]{3,1,2,0:T(8,128)} copy(f32[12,8,4,256]{3,2,1,0:T(4,128)} %bitcast.263) | data formatting | bytes 786432
  43.7 0.8 copy-done.10
  44.5 1.2 %select_add_fusion = f32[1000,128]{1,0:T(8,128)S(1)} fusion(f32[1000,128]{1,0:T(8,128)} %collective-permute-done.8, f32[1944,128]{1,0:T(8,128)S(1)} %copy-done.10, pred[]{:T(512)S(6)} %eq.17, f32[6144]{0:T(1024)S(1)} %reshape.130, f32[248832]{0:T(1024)S(1)} %reshape_reshape.3), kind=kLoop, calls=%fused_computation.63 | loop fusion | flops 896000 | bytes 2555905 | tf_op jit(solution)/shard_map/add | solution.py:39
  46.1 8.3 %collective-permute-done.9 = f32[500,128]{1,0:T(8,128)S(1)} collective-permute-done((f32[500,128]{1,0:T(8,128)S(1)}, f32[500,128]{1,0:T(8,128)S(1)}, u32[]{:S(2)}, u32[]{:S(2)}) %collective-permute-start.9) | collective-permute-done | bytes 256032 | tf_op jit(solution)/shard_map/ppermute | solution.py:28
  54.5 3.6 %collective-permute-start.10 = (f32[250,128]{1,0:T(8,128)S(1)}, f32[250,128]{1,0:T(8,128)S(1)}, u32[]{:S(2)}, u32[]{:S(2)}) collective-permute-start(f32[250,128]{1,0:T(8,128)S(1)} %slice_select_fusion.2), channel_id=1, source_target_pairs={{0,4},{4,0},{8,12},{12,8},{1,5},{5,1},{9,13},{13,9},{2,6},{6,2},{1... | collective-permute-start | bytes 384008 | tf_op jit(solution)/shard_map/ppermute | solution.py:28
  58.4 3.0 %collective-permute-done.10 = f32[250,128]{1,0:T(8,128)S(1)} collective-permute-done((f32[250,128]{1,0:T(8,128)S(1)}, f32[250,128]{1,0:T(8,128)S(1)}, u32[]{:S(2)}, u32[]{:S(2)}) %collective-permute-start.10) | collective-permute-done | bytes 128032 | tf_op jit(solution)/shard_map/ppermute | solution.py:28
  61.4 3.9 %collective-permute-start.11 = (f32[125,128]{1,0:T(8,128)S(1)}, f32[125,128]{1,0:T(8,128)S(1)}, u32[]{:S(2)}, u32[]{:S(2)}) collective-permute-start(f32[125,128]{1,0:T(8,128)S(1)} %slice_select_fusion.3), channel_id=1, source_target_pairs={{0,8},{4,12},{8,0},{12,4},{1,9},{5,13},{9,1},{13,5},{2,10},{6,14},... | collective-permute-start | bytes 192008 | tf_op jit(solution)/shard_map/ppermute | solution.py:28
  65.6 2.6 %collective-permute-done.11 = f32[125,128]{1,0:T(8,128)S(1)} collective-permute-done((f32[125,128]{1,0:T(8,128)S(1)}, f32[125,128]{1,0:T(8,128)S(1)}, u32[]{:S(2)}, u32[]{:S(2)}) %collective-permute-start.11) | collective-permute-done | bytes 64032 | tf_op jit(solution)/shard_map/ppermute | solution.py:28
  68.3 2.3 %collective-permute-start.12 = (f32[125,128]{1,0:T(8,128)S(1)}, f32[125,128]{1,0:T(8,128)S(1)}, u32[]{:S(2)}, u32[]{:S(2)}) collective-permute-start(f32[125,128]{1,0:T(8,128)S(1)} %select_add_fusion.3), channel_id=1, source_target_pairs={{0,8},{4,12},{8,0},{12,4},{1,9},{5,13},{9,1},{13,5},{2,10},{6,14},... | collective-permute-start | bytes 192008 | tf_op jit(solution)/shard_map/ppermute | solution.py:28
  70.9 3.1 %collective-permute-done.12 = f32[125,128]{1,0:T(8,128)S(1)} collective-permute-done((f32[125,128]{1,0:T(8,128)S(1)}, f32[125,128]{1,0:T(8,128)S(1)}, u32[]{:S(2)}, u32[]{:S(2)}) %collective-permute-start.12) | collective-permute-done | bytes 64032 | tf_op jit(solution)/shard_map/ppermute | solution.py:28
  74.4 4.6 %collective-permute-done.13 = f32[250,128]{1,0:T(8,128)S(1)} collective-permute-done((f32[250,128]{1,0:T(8,128)S(1)}, f32[250,128]{1,0:T(8,128)S(1)}, u32[]{:S(2)}, u32[]{:S(2)}) %collective-permute-start.13) | collective-permute-done | bytes 128032 | tf_op jit(solution)/shard_map/ppermute | solution.py:28
  79.1 0.6 collective-permute-start.14
  80.0 5.5 %collective-permute-done.14 = f32[500,128]{1,0:T(8,128)S(1)} collective-permute-done((f32[500,128]{1,0:T(8,128)S(1)}, f32[500,128]{1,0:T(8,128)S(1)}, u32[]{:S(2)}, u32[]{:S(2)}) %collective-permute-start.14) | collective-permute-done | bytes 256032 | tf_op jit(solution)/shard_map/ppermute | solution.py:28
  86.0 0.4 fusion.1
  86.5 0.7 copy.24
  87.7 1.4 %mul.50 = f32[3,3,3,96,96]{4,3,2,1,0:T(8,128)} reshape(f32[1944,128]{1,0:T(8,128)S(1)} %slice_multiply_fusion) | data formatting | bytes 1990656 | tf_op jit(solution)/shard_map/mul | solution.py:161
  89.2 0.7 copy.25
  (109 shorter events, 9.4 us)
Async XLA Ops:
  0.6 14.8 %copy-start.11 = (bf16[1,1,4,256,96]{3,4,2,1,0:T(8,128)(2,1)S(1)}, bf16[1,1,4,256,96]{3,4,2,1,0:T(8,128)(2,1)}, u32[]{:S(2)}) copy-start(bf16[1,1,4,256,96]{3,4,2,1,0:T(8,128)(2,1)} %param.5) | copy-start | bytes 589828
  0.6 21.2 %collective-permute-start.1 = (bf16[1,4,256,96]{2,3,1,0:T(8,128)(2,1)}, bf16[1,4,256,96]{2,3,1,0:T(8,128)(2,1)S(1)}, u32[]{:S(2)}, u32[]{:S(2)}) collective-permute-start(bf16[1,4,256,96]{2,3,1,0:T(8,128)(2,1)} %bitcast.246), channel_id=1, source_target_pairs={{8,0},{10,2},{12,4},{14,6},{9,1},{11,3},{13,5},{15,7},{24,16},{26,... | collective-permute-start | bytes 589832 | tf_op jit(solution)/shard_map/ppermute | solution.py:87
  2.9 17.4 %collective-permute-start = (bf16[1,1,256,96]{2,3,1,0:T(8,128)(2,1)S(1)}, bf16[1,1,256,96]{2,3,1,0:T(8,128)(2,1)S(1)}, u32[]{:S(2)}, u32[]{:S(2)}) collective-permute-start(bf16[1,1,256,96]{2,3,1,0:T(8,128)(2,1)S(1)} %get-tuple-element.44), channel_id=1, source_target_pairs={{8,2},{12,6},{9,3},{13,7},{24,18},{28,22},{25,19},{29,23}} | collective-permute-start | bytes 147464 | tf_op jit(solution)/shard_map/ppermute | solution.py:87
  3.6 12.5 %collective-permute-start.6 = (bf16[1,1,256,96]{2,3,1,0:T(8,128)(2,1)S(1)}, bf16[1,1,256,96]{2,3,1,0:T(8,128)(2,1)S(1)}, u32[]{:S(2)}, u32[]{:S(2)}) collective-permute-start(bf16[1,1,256,96]{2,3,1,0:T(8,128)(2,1)S(1)} %get-tuple-element.44), channel_id=1, source_target_pairs={{0,2},{4,6},{8,10},{12,14},{1,3},{5,7},{9,11},{13,15},{16,18},{20,... | collective-permute-start | bytes 147464 | tf_op jit(solution)/shard_map/ppermute | solution.py:87
  9.1 12.7 %collective-permute-start.2 = (bf16[1,1,256,96]{2,3,1,0:T(8,128)(2,1)S(1)}, bf16[1,1,256,96]{2,3,1,0:T(8,128)(2,1)S(1)}, u32[]{:S(2)}, u32[]{:S(2)}) collective-permute-start(bf16[1,1,256,96]{2,3,1,0:T(8,128)(2,1)S(1)} %get-tuple-element.45), channel_id=1, source_target_pairs={{10,0},{14,4},{11,1},{15,5},{26,16},{30,20},{27,17},{31,21}} | collective-permute-start | bytes 147464 | tf_op jit(solution)/shard_map/ppermute | solution.py:87
  10.4 7.0 %collective-permute-start.7 = (bf16[1,1,256,96]{2,3,1,0:T(8,128)(2,1)S(1)}, bf16[1,1,256,96]{2,3,1,0:T(8,128)(2,1)S(1)}, u32[]{:S(2)}, u32[]{:S(2)}) collective-permute-start(bf16[1,1,256,96]{2,3,1,0:T(8,128)(2,1)S(1)} %get-tuple-element.45), channel_id=1, source_target_pairs={{2,0},{6,4},{10,8},{14,12},{3,1},{7,5},{11,9},{15,13},{18,16},{22,... | collective-permute-start | bytes 147464 | tf_op jit(solution)/shard_map/ppermute | solution.py:87
  16.1 12.9 %collective-permute-start.4 = (bf16[1,4,256,96]{2,3,1,0:T(8,128)(2,1)S(1)}, bf16[1,4,256,96]{2,3,1,0:T(8,128)(2,1)S(1)}, u32[]{:S(2)}, u32[]{:S(2)}) collective-permute-start(bf16[1,4,256,96]{2,3,1,0:T(8,128)(2,1)S(1)} %bitcast.248), channel_id=1, source_target_pairs={{4,0},{6,2},{8,4},{10,6},{12,8},{14,10},{5,1},{7,3},{9,5},{11,7},{... | collective-permute-start | bytes 589832 | tf_op jit(solution)/shard_map/ppermute | solution.py:87
  17.4 6.8 %collective-permute-start.3 = (bf16[1,1,256,96]{2,3,1,0:T(8,128)(2,1)S(1)}, bf16[1,1,256,96]{2,3,1,0:T(8,128)(2,1)S(1)}, u32[]{:S(2)}, u32[]{:S(2)}) collective-permute-start(bf16[1,1,256,96]{2,3,1,0:T(8,128)(2,1)S(1)} %get-tuple-element.44), channel_id=1, source_target_pairs={{4,2},{8,6},{12,10},{5,3},{9,7},{13,11},{20,18},{24,22},{28,26},{2... | collective-permute-start | bytes 147464 | tf_op jit(solution)/shard_map/ppermute | solution.py:87
  19.1 14.7 %copy-start.12 = (bf16[1024,288]{0,1:T(8,128)(2,1)}, bf16[1024,288]{0,1:T(8,128)(2,1)S(1)}, u32[]{:S(2)}) copy-start(bf16[1024,288]{0,1:T(8,128)(2,1)S(1)} %constant_dynamic-update-slice_fusion) | copy-start | bytes 1769476
  20.3 13.9 %copy-start.14 = (bf16[36,8,4,256]{3,1,2,0:T(8,128)(2,1)}, bf16[36,8,4,256]{3,1,2,0:T(8,128)(2,1)S(1)}, u32[]{:S(2)}) copy-start(bf16[36,8,4,256]{3,1,2,0:T(8,128)(2,1)S(1)} %copy.36) | copy-start | bytes 1769476
  20.3 8.7 %collective-permute-start.5 = (bf16[1,1,256,96]{2,3,1,0:T(8,128)(2,1)S(1)}, bf16[1,1,256,96]{2,3,1,0:T(8,128)(2,1)S(1)}, u32[]{:S(2)}, u32[]{:S(2)}) collective-permute-start(bf16[1,1,256,96]{2,3,1,0:T(8,128)(2,1)S(1)} %get-tuple-element.45), channel_id=1, source_target_pairs={{6,0},{10,4},{14,8},{7,1},{11,5},{15,9},{22,16},{26,20},{30,24},{2... | collective-permute-start | bytes 147464 | tf_op jit(solution)/shard_map/ppermute | solution.py:87
  23.0 8.4 %copy-start.8 = (bf16[36,8,4,256]{3,1,2,0:T(8,128)(2,1)}, bf16[36,8,4,256]{3,1,2,0:T(8,128)(2,1)S(1)}, u32[]{:S(2)}) copy-start(bf16[36,8,4,256]{3,1,2,0:T(8,128)(2,1)S(1)} %copy.26) | copy-start | bytes 1769476
  23.6 8.2 %copy-start.2 = (bf16[36,8,4,256]{3,1,2,0:T(8,128)(2,1)}, bf16[36,8,4,256]{3,1,2,0:T(8,128)(2,1)S(1)}, u32[]{:S(2)}) copy-start(bf16[36,8,4,256]{3,1,2,0:T(8,128)(2,1)S(1)} %copy.27) | copy-start | bytes 1769476
  30.3 2.2 %copy-start.6 = (bf16[36,8,4,256]{3,1,2,0:T(8,128)(2,1)}, bf16[36,8,4,256]{3,1,2,0:T(8,128)(2,1)S(1)}, u32[]{:S(2)}) copy-start(bf16[36,8,4,256]{3,1,2,0:T(8,128)(2,1)S(1)} %copy.29) | copy-start | bytes 1769476
  30.8 2.0 %copy-start.4 = (bf16[36,8,4,256]{3,1,2,0:T(8,128)(2,1)}, bf16[36,8,4,256]{3,1,2,0:T(8,128)(2,1)S(1)}, u32[]{:S(2)}) copy-start(bf16[36,8,4,256]{3,1,2,0:T(8,128)(2,1)S(1)} %copy.30) | copy-start | bytes 1769476
  31.4 1.7 %copy-start = (bf16[36,8,4,256]{3,1,2,0:T(8,128)(2,1)}, bf16[36,8,4,256]{3,1,2,0:T(8,128)(2,1)S(1)}, u32[]{:S(2)}) copy-start(bf16[36,8,4,256]{3,1,2,0:T(8,128)(2,1)S(1)} %copy.31) | copy-start | bytes 1769476
  37.1 2.0 %copy-start.16 = (bf16[1,1,4,256,96]{3,4,2,1,0:T(8,128)(2,1)S(1)}, bf16[1,1,4,256,96]{3,4,2,1,0:T(8,128)(2,1)}, u32[]{:S(2)}) copy-start(bf16[1,1,4,256,96]{3,4,2,1,0:T(8,128)(2,1)} %param.4) | copy-start | bytes 589828
  39.0 4.6 %collective-permute-start.8 = (f32[1000,128]{1,0:T(8,128)}, f32[1000,128]{1,0:T(8,128)}, u32[]{:S(2)}, u32[]{:S(2)}) collective-permute-start(f32[1000,128]{1,0:T(8,128)} %slice_select_fusion), channel_id=1, source_target_pairs={{0,1},{1,0},{2,3},{3,2},{4,5},{5,4},{6,7},{7,6},{8,9},{9,8},{10,11... | collective-permute-start | bytes 1536008 | tf_op jit(solution)/shard_map/ppermute | solution.py:28
  41.4 1.9 %copy-start.9 = (bf16[36,8,4,256]{3,1,2,0:T(8,128)(2,1)S(1)}, bf16[36,8,4,256]{3,1,2,0:T(8,128)(2,1)}, u32[]{:S(2)}) copy-start(bf16[36,8,4,256]{3,1,2,0:T(8,128)(2,1)} %copy-done.8) | copy-start | bytes 1769476
  43.3 1.2 %copy-start.10 = (f32[1944,128]{1,0:T(8,128)S(1)}, f32[1944,128]{1,0:T(8,128)}, u32[]{:S(2)}) copy-start(f32[1944,128]{1,0:T(8,128)} %slice.223) | copy-start | bytes 2985988
  43.6 2.1 %copy-start.3 = (bf16[36,8,4,256]{3,1,2,0:T(8,128)(2,1)S(1)}, bf16[36,8,4,256]{3,1,2,0:T(8,128)(2,1)}, u32[]{:S(2)}) copy-start(bf16[36,8,4,256]{3,1,2,0:T(8,128)(2,1)} %copy-done.2) | copy-start | bytes 1769476
  45.7 8.7 %collective-permute-start.9 = (f32[500,128]{1,0:T(8,128)S(1)}, f32[500,128]{1,0:T(8,128)S(1)}, u32[]{:S(2)}, u32[]{:S(2)}) collective-permute-start(f32[500,128]{1,0:T(8,128)S(1)} %slice_select_fusion.1), channel_id=1, source_target_pairs={{0,2},{2,0},{1,3},{3,1},{4,6},{6,4},{5,7},{7,5},{8,10},{10,8},{9,1... | collective-permute-start | bytes 768008 | tf_op jit(solution)/shard_map/ppermute | solution.py:28
  54.5 10.9 %copy-start.7 = (bf16[36,8,4,256]{3,1,2,0:T(8,128)(2,1)S(1)}, bf16[36,8,4,256]{3,1,2,0:T(8,128)(2,1)}, u32[]{:S(2)}) copy-start(bf16[36,8,4,256]{3,1,2,0:T(8,128)(2,1)} %copy-done.6) | copy-start | bytes 1769476
  54.5 6.9 %collective-permute-start.10 = (f32[250,128]{1,0:T(8,128)S(1)}, f32[250,128]{1,0:T(8,128)S(1)}, u32[]{:S(2)}, u32[]{:S(2)}) collective-permute-start(f32[250,128]{1,0:T(8,128)S(1)} %slice_select_fusion.2), channel_id=1, source_target_pairs={{0,4},{4,0},{8,12},{12,8},{1,5},{5,1},{9,13},{13,9},{2,6},{6,2},{1... | collective-permute-start | bytes 384008 | tf_op jit(solution)/shard_map/ppermute | solution.py:28
  58.4 12.2 %copy-start.5 = (bf16[36,8,4,256]{3,1,2,0:T(8,128)(2,1)S(1)}, bf16[36,8,4,256]{3,1,2,0:T(8,128)(2,1)}, u32[]{:S(2)}) copy-start(bf16[36,8,4,256]{3,1,2,0:T(8,128)(2,1)} %copy-done.4) | copy-start | bytes 1769476
  61.4 6.8 %collective-permute-start.11 = (f32[125,128]{1,0:T(8,128)S(1)}, f32[125,128]{1,0:T(8,128)S(1)}, u32[]{:S(2)}, u32[]{:S(2)}) collective-permute-start(f32[125,128]{1,0:T(8,128)S(1)} %slice_select_fusion.3), channel_id=1, source_target_pairs={{0,8},{4,12},{8,0},{12,4},{1,9},{5,13},{9,1},{13,5},{2,10},{6,14},... | collective-permute-start | bytes 192008 | tf_op jit(solution)/shard_map/ppermute | solution.py:28
  65.6 8.5 %copy-start.1 = (bf16[36,8,4,256]{3,1,2,0:T(8,128)(2,1)S(1)}, bf16[36,8,4,256]{3,1,2,0:T(8,128)(2,1)}, u32[]{:S(2)}) copy-start(bf16[36,8,4,256]{3,1,2,0:T(8,128)(2,1)} %copy-done) | copy-start | bytes 1769476
  68.3 5.7 %collective-permute-start.12 = (f32[125,128]{1,0:T(8,128)S(1)}, f32[125,128]{1,0:T(8,128)S(1)}, u32[]{:S(2)}, u32[]{:S(2)}) collective-permute-start(f32[125,128]{1,0:T(8,128)S(1)} %select_add_fusion.3), channel_id=1, source_target_pairs={{0,8},{4,12},{8,0},{12,4},{1,9},{5,13},{9,1},{13,5},{2,10},{6,14},... | collective-permute-start | bytes 192008 | tf_op jit(solution)/shard_map/ppermute | solution.py:28
  74.0 5.0 %collective-permute-start.13 = (f32[250,128]{1,0:T(8,128)S(1)}, f32[250,128]{1,0:T(8,128)S(1)}, u32[]{:S(2)}, u32[]{:S(2)}) collective-permute-start(f32[250,128]{1,0:T(8,128)S(1)} %maximum_select_fusion.3), channel_id=1, source_target_pairs={{0,4},{4,0},{8,12},{12,8},{1,5},{5,1},{9,13},{13,9},{2,6},{6,2},{1... | collective-permute-start | bytes 384008 | tf_op jit(solution)/shard_map/ppermute | solution.py:28
  79.1 6.4 %collective-permute-start.14 = (f32[500,128]{1,0:T(8,128)S(1)}, f32[500,128]{1,0:T(8,128)S(1)}, u32[]{:S(2)}, u32[]{:S(2)}) collective-permute-start(f32[500,128]{1,0:T(8,128)S(1)} %maximum_select_fusion.2), channel_id=1, source_target_pairs={{0,2},{2,0},{1,3},{3,1},{4,6},{6,4},{5,7},{7,5},{8,10},{10,8},{9,1... | collective-permute-start | bytes 768008 | tf_op jit(solution)/shard_map/ppermute | solution.py:28
  79.7 6.0 %copy-start.13 = (bf16[1024,288]{0,1:T(8,128)(2,1)S(1)}, bf16[1024,288]{0,1:T(8,128)(2,1)}, u32[]{:S(2)}) copy-start(bf16[1024,288]{0,1:T(8,128)(2,1)} %copy-done.12) | copy-start | bytes 1769476
  80.0 6.0 %copy-start.15 = (bf16[36,8,4,256]{3,1,2,0:T(8,128)(2,1)S(1)}, bf16[36,8,4,256]{3,1,2,0:T(8,128)(2,1)}, u32[]{:S(2)}) copy-start(bf16[36,8,4,256]{3,1,2,0:T(8,128)(2,1)} %copy-done.14) | copy-start | bytes 1769476
  80.0 6.0 %copy-start.17 = (f32[12,8,4,256]{3,1,2,0:T(8,128)S(1)}, f32[12,8,4,256]{3,1,2,0:T(8,128)}, u32[]{:S(2)}) copy-start(f32[12,8,4,256]{3,1,2,0:T(8,128)} %copy.37) | copy-start | bytes 1179652
  85.5 2.0 %collective-permute-start.15 = (f32[1000,128]{1,0:T(8,128)S(1)}, f32[1000,128]{1,0:T(8,128)S(1)}, u32[]{:S(2)}, u32[]{:S(2)}) collective-permute-start(f32[1000,128]{1,0:T(8,128)S(1)} %maximum_select_fusion.1), channel_id=1, source_target_pairs={{0,1},{1,0},{2,3},{3,2},{4,5},{5,4},{6,7},{7,6},{8,9},{9,8},{10,11... | collective-permute-start | bytes 1536008 | tf_op jit(solution)/shard_map/ppermute | solution.py:28
